TPU v7x, 128 devices: a whole 4x4x4 slice. The times are simulated.
128 devices in a mesh: seq: 32 (over y, x, core), mp: 4 (over z).
Axes of the slice: x: 4, y: 4, z: 4, core: 2. Of those that a mesh axis runs over, the one named last changes fastest.
Arguments:
- states: bfloat16 [4, 16, 2048], P(None, None, 'mp'), may hold values from -4 to 4
- query_weight: bfloat16 [2048, 2048], P('seq', 'mp'), may hold values from -5 to 5
- key_weight: bfloat16 [2048, 2048], P('seq', 'mp'), may hold values from -5 to 5
- value_weight: bfloat16 [2048, 2048], P('seq', 'mp'), may hold values from -5 to 5
- output_weight: bfloat16 [2048, 2048], P('seq', 'mp'), may hold values from -5 to 5
- gate_weight: bfloat16 [2048, 8192], P('seq', 'mp'), may hold values from -5 to 5
- up_weight: bfloat16 [2048, 8192], P('seq', 'mp'), may hold values from -5 to 5
- down_weight: bfloat16 [8192, 2048], P('seq', 'mp'), may hold values from -5 to 5
- query_gain: float32 [2048], P('mp'), may hold values from 0.5 to 2
- key_gain: float32 [2048], P('mp'), may hold values from 0.5 to 2
- attention_gain: float32 [2048], P('mp'), may hold values from 0.1 to 1.9
- feedforward_gain: float32 [2048], P('mp'), may hold values from 0.1 to 1.9
- key_cache: bfloat16 [512, 256, 2048], P('seq', None, 'mp'), may hold values from -500 to 500
- value_cache: bfloat16 [512, 256, 2048], P('seq', None, 'mp'), may hold values from -6 to 6
- lengths: int32 [16], replicated, may hold values from 1 to 32768, as said below
- page_owner: int32 [512], P('seq'), may hold values from -1 to 15, as said below
- page_index: int32 [512], P('seq'), may hold values from 0 to 127, as said below
Outputs:
- decoded: bfloat16 [4, 16, 2048], P(None, None, 'mp')
Inputs may be any that keep to these rules, and one draw needn't show every extreme that they name: Request r owns exactly ceil(lengths[r] / 256) pages. `page_owner`: on each device of seq the used pages come before the unused ones. `page_index`: the pages of one request carry the numbers 0, 1, 2 and so on, once each; unused pages carry 0.
All inputs are finite; a program needn't handle non-finite values.
Results may differ from a plain program's by a relative error of at most 0.015.
Values may be sent and summed in bfloat16 or wider, within the bound.
No kernel may reach another device: no remote copies, remote signals or barrier semaphores. Data moves between devices by JAX's collectives and lax.ppermute only.
A program may use at most 64 MiB of HBM per device.

v0:
```python
import jax
import jax.numpy as jnp
from jax import lax
from jax.sharding import PartitionSpec as P

D = 2048
HD = 128
R = 16
STEPS = 4
PAGE = 256


epsilon = 1e-06
rope_base = 500000.0
very_low = -1e30
exact_mode = lax.Precision.HIGHEST
pages_per_block = 4


def combined_all(value, axis, join):
    pieces = jax.tree.map(lambda part: lax.all_gather(part, axis), value)
    head = jax.tree.map(lambda part: part[0], pieces)
    tail = jax.tree.map(lambda part: part[1:], pieces)
    subtotal, _ = lax.scan(lambda subtotal, piece: (join(subtotal, piece), None), head, tail)
    return subtotal


def rotary(values, positions):
    half_width = HD // 2
    frequencies = rope_base ** (-2.0 * jnp.arange(half_width, dtype=jnp.float32) / HD)
    angles = positions.astype(jnp.float32)[:, None] * frequencies[None, :]
    cosine = jnp.cos(angles)[:, None, :]
    sine_part = jnp.sin(angles)[:, None, :]
    first_half = values[..., :half_width]
    second_half = values[..., half_width:]
    return jnp.concatenate(
        [
            first_half * cosine - second_half * sine_part,
            second_half * cosine + first_half * sine_part,
        ],
        axis=-1,
    )


def seq_columns(token_rows, width):
    gathered = lax.all_gather(token_rows, "mp", axis=1, tiled=True)
    return lax.dynamic_slice_in_dim(gathered, lax.axis_index("seq") * width, width, 1)


def seq_total(partial_value):
    return lax.psum(partial_value, "seq")


def feature_sums(squares):
    return lax.psum(squares, "mp")


def inverse_rms(square_total):
    return lax.rsqrt(square_total / D + epsilon)[:, None]


def combine_parts(earlier, later_part):
    highest = jnp.maximum(earlier[0], later_part[0])
    first_scale = jnp.exp(earlier[0] - highest)
    second_scale = jnp.exp(later_part[0] - highest)
    return (
        highest,
        earlier[1] * first_scale + later_part[1] * second_scale,
        earlier[2] * first_scale[..., None] + later_part[2] * second_scale[..., None],
    )


def local(
    states,
    query_weight,
    key_weight,
    value_weight,
    output_weight,
    gate_weight,
    up_weight,
    down_weight,
    query_gain,
    key_gain,
    attention_gain,
    feedforward_gain,
    key_cache,
    value_cache,
    lengths,
    page_owner,
    page_index,
):
    local_width = query_weight.shape[1]
    local_heads = local_width // HD
    requests = jnp.arange(R, dtype=jnp.int32)
    score_scale = HD ** (-0.5)
    outputs = []
    key_list = []
    value_list = []
    for step_index in range(STEPS):
        token_rows = states[step_index]
        positions = lengths + step_index
        attention_row_count = token_rows.shape[0]
        attention_sliced = seq_columns(token_rows, query_weight.shape[0])
        partial_value = jnp.concatenate(
            [
                jnp.dot(attention_sliced, query_weight, preferred_element_type=jnp.float32),
                jnp.dot(attention_sliced, key_weight, preferred_element_type=jnp.float32),
                jnp.dot(attention_sliced, value_weight, preferred_element_type=jnp.float32),
            ],
            axis=1,
        )
        summed = seq_total(partial_value)
        query_raw = summed[:, :local_width]
        key_raw = summed[:, local_width : 2 * local_width]
        value_raw = summed[:, 2 * local_width :]
        squares = feature_sums(
            jnp.stack(
                [jnp.sum(query_raw * query_raw, axis=1), jnp.sum(key_raw * key_raw, axis=1)], axis=1
            )
        )
        attention_queries = query_raw * inverse_rms(squares[:, 0]) * query_gain
        attention_new_keys = key_raw * inverse_rms(squares[:, 1]) * key_gain
        attention_queries = rotary(
            attention_queries.reshape(attention_row_count, local_heads, HD), positions
        ).astype(jnp.bfloat16)
        attention_new_keys = rotary(
            attention_new_keys.reshape(attention_row_count, local_heads, HD), positions
        ).astype(jnp.bfloat16)
        attention_new_values = value_raw.astype(jnp.bfloat16).reshape(
            attention_row_count, local_heads, HD
        )
        key_list.append(attention_new_keys[None])
        value_list.append(attention_new_values[None])
        cache_queries = attention_queries[None]
        steps_here = cache_queries.shape[0]

        def fold_block(block_index, carried):
            maxima, totals, running = carried
            first_page = block_index * pages_per_block
            key_block = lax.dynamic_slice_in_dim(key_cache, first_page, pages_per_block, 0).reshape(
                pages_per_block, PAGE, local_heads, HD
            )
            value_block = lax.dynamic_slice_in_dim(
                value_cache, first_page, pages_per_block, 0
            ).reshape(pages_per_block, PAGE, local_heads, HD)
            owners = lax.dynamic_slice_in_dim(page_owner, first_page, pages_per_block, 0)
            indices = lax.dynamic_slice_in_dim(page_index, first_page, pages_per_block, 0)
            matches = owners[:, None] == requests[None, :]
            onehot = matches.astype(jnp.float32)
            picked = jnp.take(cache_queries, jnp.maximum(owners, 0), axis=1)
            scores = (
                jnp.einsum("sghd,gthd->sgth", picked, key_block, preferred_element_type=jnp.float32)
                * score_scale
            )
            page_lengths = jnp.sum(jnp.where(matches, lengths[None, :], 0), axis=1)
            token_spots = indices[:, None] * PAGE + jnp.arange(PAGE, dtype=jnp.int32)[None, :]
            validity = (token_spots < page_lengths[:, None])[None, :, :, None]
            masked = jnp.where(validity, scores, very_low)
            page_top = jnp.max(masked, axis=2)
            request_top = jnp.max(
                jnp.where(matches.T[None, :, :, None], page_top[:, None, :, :], very_low), axis=2
            )
            highest = jnp.maximum(maxima, request_top)
            page_ref = jnp.take(highest, jnp.maximum(owners, 0), axis=1)
            weights = jnp.where(validity, jnp.exp(masked - page_ref[:, :, None, :]), 0.0)
            page_total = jnp.sum(weights, axis=2)
            page_sum = jnp.einsum(
                "sgth,gthd->sghd",
                weights.astype(jnp.bfloat16),
                value_block,
                preferred_element_type=jnp.float32,
            )
            factor = jnp.exp(maxima - highest)
            totals = totals * factor + jnp.einsum(
                "gr,sgh->srh", onehot, page_total, precision=exact_mode
            )
            running = running * factor[..., None] + jnp.einsum(
                "gr,sghd->srhd", onehot, page_sum, precision=exact_mode
            )
            return (highest, totals, running)

        block_count = page_owner.shape[0] // pages_per_block
        initial = (
            jnp.full((steps_here, R, local_heads), very_low, jnp.float32),
            jnp.zeros((steps_here, R, local_heads), jnp.float32),
            jnp.zeros((steps_here, R, local_heads, HD), jnp.float32),
        )
        maxima, totals, running = lax.fori_loop(0, block_count, fold_block, initial)
        merged_parts = combined_all((maxima, totals, running), "seq", combine_parts)
        finish_queries = attention_queries[None]
        finish_new_keys = jnp.concatenate(key_list, axis=0)
        finish_maxima, finish_totals, finish_running = merged_parts
        finish_steps_here = finish_queries.shape[0]
        known = finish_new_keys.shape[0]
        fresh_scores = (
            jnp.einsum(
                "srhd,trhd->srht",
                finish_queries,
                finish_new_keys,
                preferred_element_type=jnp.float32,
            )
            * score_scale
        )
        allowed = (
            jnp.arange(known)[None, :] <= step_index + jnp.arange(finish_steps_here)[:, None]
        )[:, None, None, :]
        fresh_scores = jnp.where(allowed, fresh_scores, very_low)
        finish_highest = jnp.maximum(finish_maxima, jnp.max(fresh_scores, axis=-1))
        fresh_weights = jnp.where(allowed, jnp.exp(fresh_scores - finish_highest[..., None]), 0.0)
        finish_factor = jnp.exp(finish_maxima - finish_highest)
        finish_totals = finish_totals * finish_factor + jnp.sum(fresh_weights, axis=-1)
        finish_running = finish_running * finish_factor[..., None] + jnp.einsum(
            "srht,trhd->srhd",
            fresh_weights.astype(jnp.bfloat16),
            jnp.concatenate(value_list, axis=0),
            preferred_element_type=jnp.float32,
        )
        attended = (finish_running / finish_totals[..., None]).astype(jnp.bfloat16)
        layer_attended = attended.reshape(R, local_width)
        sliced = seq_columns(layer_attended, output_weight.shape[0])
        attention_out = seq_total(
            jnp.dot(sliced, output_weight, preferred_element_type=jnp.float32)
        )
        attention_squares = feature_sums(
            jnp.sum(attention_out * attention_out, axis=1, keepdims=True)
        )
        hidden = (
            token_rows.astype(jnp.float32)
            + attention_out * inverse_rms(attention_squares[:, 0]) * attention_gain
        ).astype(jnp.bfloat16)
        hidden_cols = seq_columns(hidden, gate_weight.shape[0])
        gate_part = jnp.dot(hidden_cols, gate_weight, preferred_element_type=jnp.float32)
        up_part = jnp.dot(hidden_cols, up_weight, preferred_element_type=jnp.float32)
        hidden_units = gate_weight.shape[1]
        summed_both = seq_total(jnp.concatenate([gate_part, up_part], axis=1))
        active = (
            jax.nn.silu(summed_both[:, :hidden_units]) * summed_both[:, hidden_units:]
        ).astype(jnp.bfloat16)
        active_cols = seq_columns(active, down_weight.shape[0])
        mlp_out = seq_total(jnp.dot(active_cols, down_weight, preferred_element_type=jnp.float32))
        mlp_squares = feature_sums(jnp.sum(mlp_out * mlp_out, axis=1, keepdims=True))
        outputs.append(
            (
                hidden.astype(jnp.float32)
                + mlp_out * inverse_rms(mlp_squares[:, 0]) * feedforward_gain
            ).astype(jnp.bfloat16)
        )
    return jnp.stack(outputs, axis=0)


def solution(mesh):
    in_specs = (
        P(None, None, "mp"),
        P("seq", "mp"),
        P("seq", "mp"),
        P("seq", "mp"),
        P("seq", "mp"),
        P("seq", "mp"),
        P("seq", "mp"),
        P("seq", "mp"),
        P("mp"),
        P("mp"),
        P("mp"),
        P("mp"),
        P("seq", None, "mp"),
        P("seq", None, "mp"),
        P(),
        P("seq"),
        P("seq"),
    )
    out_specs = P(None, None, "mp")
    return jax.shard_map(local, mesh=mesh, in_specs=in_specs, out_specs=out_specs, check_vma=False)
```

profile of v0, /device:TPU:0, one launch (start us, length us, event | category | flops | bytes accessed | tf_op | source)
XLA Modules:
  0.0 1058.3 jit_solution(6257620773819369397)
XLA Ops:
  7.4 13.2 %all-gather = bf16[1,16,2048]{2,1,0:T(8,128)(2,1)S(1)} all-gather(bf16[1,16,512]{2,1,0:T(8,128)(2,1)S(1)} %get-tuple-element.1524), channel_id=2, replica_groups=mesh['seq'=32,'mp'=4] {'mp'}, dimensions={2}, use_global_device_ids=true | all-gather | bytes 81920 | tf_op jit(solution)/shard_map/all_gather | solution.py:46
  22.6 11.9 %all-gather.12 = bf16[1,16,2048]{2,1,0:T(8,128)(2,1)S(1)} all-gather(bf16[1,16,512]{2,1,0:T(8,128)(2,1)S(1)} %get-tuple-element.1525), channel_id=14, replica_groups=mesh['seq'=32,'mp'=4] {'mp'}, dimensions={2}, use_global_device_ids=true | all-gather | bytes 81920 | tf_op jit(solution)/shard_map/all_gather | solution.py:46
  38.6 11.9 %all-gather.8 = bf16[1,16,2048]{2,1,0:T(8,128)(2,1)S(1)} all-gather(bf16[1,16,512]{2,1,0:T(8,128)(2,1)S(1)} %get-tuple-element.1526), channel_id=10, replica_groups=mesh['seq'=32,'mp'=4] {'mp'}, dimensions={2}, use_global_device_ids=true | all-gather | bytes 81920 | tf_op jit(solution)/shard_map/all_gather | solution.py:46
  53.6 11.9 %all-gather.4 = bf16[1,16,2048]{2,1,0:T(8,128)(2,1)S(1)} all-gather(bf16[1,16,512]{2,1,0:T(8,128)(2,1)S(1)} %get-tuple-element.1523), channel_id=6, replica_groups=mesh['seq'=32,'mp'=4] {'mp'}, dimensions={2}, use_global_device_ids=true | all-gather | bytes 81920 | tf_op jit(solution)/shard_map/all_gather | solution.py:46
  72.2 103.9 %all-reduce.18.cloned.1.call-done = (f32[16,1536]{1,0:T(8,128)}, f32[16,1536]{1,0:T(8,128)}, f32[16,1536]{1,0:T(8,128)}, f32[16,1536]{1,0:T(8,128)}) async-done(((f32[16,1536]{1,0:T(8,128)}, f32[16,1536]{1,0:T(8,128)}, f32[16,1536]{1,0:T(8,128)}, f32[16,1536]{1,0:T(8,128)}), (f32[16,1536]{1,0:T(8,128)}, f32[16,1536]{1,0:T(8,128)}, f32[16,1536]{1,0:T(8,128)}, ...) | async-done | bytes 393232 | tf_op jit(solution)/shard_map/psum | solution.py:51
  178.1 10.7 %all-reduce.6 = (f32[16,2]{0,1:T(2,128)S(1)}, f32[16,2]{0,1:T(2,128)S(1)}, f32[16,2]{0,1:T(2,128)S(1)}, f32[16,2]{0,1:T(2,128)S(1)}) all-reduce(f32[16,2]{0,1:T(2,128)S(1)} %pad_maximum_fusion.19, f32[16,2]{0,1:T(2,128)S(1)} %pad_maximum_fusion.18, f32[16,2]{0,1:T(2,128)S(1)} %pad_maximum_fusion.17, ...), channel_id=1, replica_groups=mesh['seq'=32,'mp'=4] {'mp'}, use_global_device_ids=true, to_apply=%region_64.67 | all-reduce | flops 128 | bytes 1024 | tf_op jit(solution)/shard_map/psum | solution.py:55
  190.2 26.4 %while.139 = (s32[]{:T(128)}, f32[1,16,4]{1,2,0:T(4,128)S(1)}, f32[1,16,4]{1,2,0:T(4,128)S(1)}, f32[1,16,4,128]{3,1,2,0:T(8,128)S(1)}, s32[16]{0:T(128)S(1)}, /*...) while((s32[]{:T(128)}, f32[1,16,4]{1,2,0:T(4,128)S(1)}, ...), condition=%wide.region_70.73_spmd.clone.clone, body=%wide.region_65.72_spmd.clone.clone.sunk | while | flops 2561347 | bytes 6471395 | solution.py:188
  190.9 1.6 fusion.416
  194.2 1.3 constant_dynamic-slice_fusion.51
  197.5 1.6 fusion.416
  200.8 1.3 constant_dynamic-slice_fusion.51
  204.1 1.6 fusion.416
  207.4 1.3 constant_dynamic-slice_fusion.51
  210.7 1.6 fusion.416
  214.0 1.3 constant_dynamic-slice_fusion.51
  217.5 26.4 %while.138 = (s32[]{:T(128)}, f32[1,16,4]{1,2,0:T(4,128)S(1)}, f32[1,16,4]{1,2,0:T(4,128)S(1)}, f32[1,16,4,128]{3,1,2,0:T(8,128)S(1)}, s32[16]{0:T(128)S(1)}, /*...) while((s32[]{:T(128)}, f32[1,16,4]{1,2,0:T(4,128)S(1)}, ...), condition=%wide.region_49.52_spmd.clone.clone, body=%wide.region_44.51_spmd.clone.clone.sunk | while | flops 2561347 | bytes 6471395 | solution.py:188
  218.3 1.6 fusion.401
  224.9 1.6 fusion.401
  228.2 1.3 constant_dynamic-slice_fusion.50
  231.4 1.6 fusion.401
  234.8 1.3 constant_dynamic-slice_fusion.50
  238.0 1.6 fusion.401
  244.5 26.4 %while.137 = (s32[]{:T(128)}, f32[1,16,4]{1,2,0:T(4,128)S(1)}, f32[1,16,4]{1,2,0:T(4,128)S(1)}, f32[1,16,4,128]{3,1,2,0:T(8,128)S(1)}, s32[16]{0:T(128)S(1)}, /*...) while((s32[]{:T(128)}, f32[1,16,4]{1,2,0:T(4,128)S(1)}, ...), condition=%wide.region_28.31_spmd.clone.clone, body=%wide.region_23.30_spmd.clone.clone.sunk | while | flops 2561347 | bytes 6471395 | solution.py:188
  245.2 1.6 fusion.386
  248.5 1.3 constant_dynamic-slice_fusion.49
  251.8 1.6 fusion.386
  258.4 1.6 fusion.386
  265.0 1.6 fusion.386
  271.4 26.3 %while.136 = (s32[]{:T(128)}, f32[1,16,4]{1,2,0:T(4,128)S(1)}, f32[1,16,4]{1,2,0:T(4,128)S(1)}, f32[1,16,4,128]{3,1,2,0:T(8,128)S(1)}, s32[16]{0:T(128)S(1)}, /*...) while((s32[]{:T(128)}, f32[1,16,4]{1,2,0:T(4,128)S(1)}, ...), condition=%wide.region_9.12_spmd.clone.clone, body=%wide.region_4.11_spmd.clone.clone.sunk | while | flops 2561347 | bytes 6471395 | solution.py:188
  272.2 1.6 fusion.371
  278.8 1.6 fusion.371
  285.4 1.6 fusion.371
  291.9 1.6 fusion.371
  300.9 24.7 %all-gather.13 = f32[32,16,4]{1,2,0:T(4,128)S(1)} all-gather(f32[1,16,4]{1,2,0:T(4,128)S(1)} %get-tuple-element.937), channel_id=15, replica_groups=mesh['seq'=32,'mp'=4] {'seq'}, dimensions={0}, use_global_device_ids=true | all-gather | bytes 8448 | tf_op jit(solution)/shard_map/all_gather | solution.py:21
  325.5 21.5 %all-gather.14 = f32[32,16,4]{1,2,0:T(4,128)S(1)} all-gather(f32[1,16,4]{1,2,0:T(4,128)S(1)} %get-tuple-element.938), channel_id=16, replica_groups=mesh['seq'=32,'mp'=4] {'seq'}, dimensions={0}, use_global_device_ids=true | all-gather | bytes 8448 | tf_op jit(solution)/shard_map/all_gather | solution.py:21
  347.6 24.0 %all-gather.9 = f32[32,16,4]{1,2,0:T(4,128)S(1)} all-gather(f32[1,16,4]{1,2,0:T(4,128)S(1)} %get-tuple-element.931), channel_id=11, replica_groups=mesh['seq'=32,'mp'=4] {'seq'}, dimensions={0}, use_global_device_ids=true | all-gather | bytes 8448 | tf_op jit(solution)/shard_map/all_gather | solution.py:21
  371.7 21.5 %all-gather.10 = f32[32,16,4]{1,2,0:T(4,128)S(1)} all-gather(f32[1,16,4]{1,2,0:T(4,128)S(1)} %get-tuple-element.932), channel_id=12, replica_groups=mesh['seq'=32,'mp'=4] {'seq'}, dimensions={0}, use_global_device_ids=true | all-gather | bytes 8448 | tf_op jit(solution)/shard_map/all_gather | solution.py:21
  393.7 24.0 %all-gather.5 = f32[32,16,4]{1,2,0:T(4,128)S(1)} all-gather(f32[1,16,4]{1,2,0:T(4,128)S(1)} %get-tuple-element.925), channel_id=7, replica_groups=mesh['seq'=32,'mp'=4] {'seq'}, dimensions={0}, use_global_device_ids=true | all-gather | bytes 8448 | tf_op jit(solution)/shard_map/all_gather | solution.py:21
  417.8 21.5 %all-gather.6 = f32[32,16,4]{1,2,0:T(4,128)S(1)} all-gather(f32[1,16,4]{1,2,0:T(4,128)S(1)} %get-tuple-element.926), channel_id=8, replica_groups=mesh['seq'=32,'mp'=4] {'seq'}, dimensions={0}, use_global_device_ids=true | all-gather | bytes 8448 | tf_op jit(solution)/shard_map/all_gather | solution.py:21
  439.8 24.0 %all-gather.1 = f32[32,16,4]{1,2,0:T(4,128)S(1)} all-gather(f32[1,16,4]{1,2,0:T(4,128)S(1)} %get-tuple-element.919), channel_id=3, replica_groups=mesh['seq'=32,'mp'=4] {'seq'}, dimensions={0}, use_global_device_ids=true | all-gather | bytes 8448 | tf_op jit(solution)/shard_map/all_gather | solution.py:21
  463.8 21.5 %all-gather.2 = f32[32,16,4]{1,2,0:T(4,128)S(1)} all-gather(f32[1,16,4]{1,2,0:T(4,128)S(1)} %get-tuple-element.920), channel_id=4, replica_groups=mesh['seq'=32,'mp'=4] {'seq'}, dimensions={0}, use_global_device_ids=true | all-gather | bytes 8448 | tf_op jit(solution)/shard_map/all_gather | solution.py:21
  488.8 12.3 %while.135 = (s32[]{:T(128)}, f32[1,16,4]{1,2,0:T(4,128)S(1)}, f32[1,16,4]{1,2,0:T(4,128)S(1)}, f32[1,16,4,128]{3,2,1,0:T(4,128)S(1)}, f32[31,1,16,4]{2,3,1,0:T(...) while((s32[]{:T(128)}, f32[1,16,4]{1,2,0:T(4,128)S(1)}, ...), condition=%wide.region_72.75_spmd, body=%wide.region_71.74_spmd.sunk | while | flops 25026 | bytes 168809 | solution.py:24
  502.3 1.3 slice_bitcast_fusion.1
  503.6 12.3 %while.134 = (s32[]{:T(128)}, f32[1,16,4]{1,2,0:T(4,128)S(1)}, f32[1,16,4]{1,2,0:T(4,128)S(1)}, f32[1,16,4,128]{3,2,1,0:T(4,128)S(1)}, f32[31,1,16,4]{2,3,1,0:T(...) while((s32[]{:T(128)}, f32[1,16,4]{1,2,0:T(4,128)S(1)}, ...), condition=%wide.region_51.54_spmd, body=%wide.region_50.53_spmd.sunk | while | flops 25026 | bytes 168809 | solution.py:24
  516.2 9.7 all-gather.23.cloned.1.call-done
  528.1 12.3 %while.133 = (s32[]{:T(128)}, f32[1,16,4]{1,2,0:T(4,128)S(1)}, f32[1,16,4]{1,2,0:T(4,128)S(1)}, f32[1,16,4,128]{3,2,1,0:T(4,128)S(1)}, f32[31,1,16,4]{2,3,1,0:T(...) while((s32[]{:T(128)}, f32[1,16,4]{1,2,0:T(4,128)S(1)}, ...), condition=%wide.region_30.33_spmd, body=%wide.region_29.32_spmd.sunk | while | flops 25026 | bytes 168809 | solution.py:24
  541.9 12.3 %all_gather.157 = bf16[16,2048]{1,0:T(8,128)(2,1)S(1)} all-gather(bf16[16,512]{1,0:T(8,128)(2,1)S(1)} %bitcast.1038), channel_id=1, replica_groups=mesh['seq'=32,'mp'=4] {'mp'}, dimensions={1}, use_global_device_ids=true | all-gather | bytes 81920 | tf_op jit(solution)/shard_map/all_gather | solution.py:46
  554.2 11.9 %all_gather.147 = bf16[16,2048]{1,0:T(8,128)(2,1)S(1)} all-gather(bf16[16,512]{1,0:T(8,128)(2,1)S(1)} %bitcast.1039), channel_id=1, replica_groups=mesh['seq'=32,'mp'=4] {'mp'}, dimensions={1}, use_global_device_ids=true | all-gather | bytes 81920 | tf_op jit(solution)/shard_map/all_gather | solution.py:46
  566.2 11.9 %all_gather.137 = bf16[16,2048]{1,0:T(8,128)(2,1)S(1)} all-gather(bf16[16,512]{1,0:T(8,128)(2,1)S(1)} %bitcast.1040), channel_id=1, replica_groups=mesh['seq'=32,'mp'=4] {'mp'}, dimensions={1}, use_global_device_ids=true | all-gather | bytes 81920 | tf_op jit(solution)/shard_map/all_gather | solution.py:46
  582.5 12.3 %while.132 = (s32[]{:T(128)}, f32[1,16,4]{1,2,0:T(4,128)S(1)}, f32[1,16,4]{1,2,0:T(4,128)S(1)}, f32[1,16,4,128]{3,2,1,0:T(4,128)S(1)}, f32[31,1,16,4]{2,3,1,0:T(...) while((s32[]{:T(128)}, f32[1,16,4]{1,2,0:T(4,128)S(1)}, ...), condition=%wide.region_11.14_spmd, body=%wide.region_10.13_spmd.sunk | while | flops 25026 | bytes 168809 | solution.py:24
  595.2 11.9 %all_gather.127 = bf16[16,2048]{1,0:T(8,128)(2,1)S(1)} all-gather(bf16[16,512]{1,0:T(8,128)(2,1)S(1)} %bitcast.1041), channel_id=1, replica_groups=mesh['seq'=32,'mp'=4] {'mp'}, dimensions={1}, use_global_device_ids=true | all-gather | bytes 81920 | tf_op jit(solution)/shard_map/all_gather | solution.py:46
  607.9 100.2 %all-reduce.14.cloned.1.call-done = (f32[16,512]{1,0:T(8,128)}, f32[16,512]{1,0:T(8,128)}, f32[16,512]{1,0:T(8,128)}, f32[16,512]{1,0:T(8,128)}) async-done(((f32[16,512]{1,0:T(8,128)}, f32[16,512]{1,0:T(8,128)}, f32[16,512]{1,0:T(8,128)}, f32[16,512]{1,0:T(8,128)}), (f32[16,512]{1,0:T(8,128)}, f32[16,512]{1,0:T(8,128)}, f32[16,512]{1,0:T(8,128)}, f32[16,512]{1,0:T(8,128)})) %all-reduce.14.cloned.1.call-update) | async-done | bytes 131088 | tf_op jit(solution)/shard_map/psum | solution.py:51
  711.6 10.7 %all-reduce.5 = (f32[16,1]{0,1:T(1,128)S(1)}, f32[16,1]{0,1:T(1,128)S(1)}, f32[16,1]{0,1:T(1,128)S(1)}, f32[16,1]{0,1:T(1,128)S(1)}) all-reduce(f32[16,1]{0,1:T(1,128)S(1)} %bitcast.1049, f32[16,1]{0,1:T(1,128)S(1)} %bitcast.1050, f32[16,1]{0,1:T(1,128)S(1)} %bitcast.1051, ...), channel_id=1, replica_groups=mesh['seq'=32,'mp'=4] {'mp'}, use_global_device_ids=true, to_apply=%region_77.80 | all-reduce | flops 64 | bytes 512 | tf_op jit(solution)/shard_map/psum | solution.py:55
  723.3 11.9 %all_gather.158 = bf16[16,2048]{1,0:T(8,128)(2,1)S(1)} all-gather(bf16[16,512]{1,0:T(8,128)(2,1)S(1)} %get-tuple-element.1522), channel_id=1, replica_groups=mesh['seq'=32,'mp'=4] {'mp'}, dimensions={1}, use_global_device_ids=true | all-gather | bytes 81920 | tf_op jit(solution)/shard_map/all_gather | solution.py:46
  735.6 11.9 %all_gather.148 = bf16[16,2048]{1,0:T(8,128)(2,1)S(1)} all-gather(bf16[16,512]{1,0:T(8,128)(2,1)S(1)} %get-tuple-element.1521), channel_id=1, replica_groups=mesh['seq'=32,'mp'=4] {'mp'}, dimensions={1}, use_global_device_ids=true | all-gather | bytes 81920 | tf_op jit(solution)/shard_map/all_gather | solution.py:46
  747.9 11.9 %all_gather.138 = bf16[16,2048]{1,0:T(8,128)(2,1)S(1)} all-gather(bf16[16,512]{1,0:T(8,128)(2,1)S(1)} %get-tuple-element.1520), channel_id=1, replica_groups=mesh['seq'=32,'mp'=4] {'mp'}, dimensions={1}, use_global_device_ids=true | all-gather | bytes 81920 | tf_op jit(solution)/shard_map/all_gather | solution.py:46
  760.2 12.0 %all_gather.128 = bf16[16,2048]{1,0:T(8,128)(2,1)S(1)} all-gather(bf16[16,512]{1,0:T(8,128)(2,1)S(1)} %get-tuple-element.1519), channel_id=1, replica_groups=mesh['seq'=32,'mp'=4] {'mp'}, dimensions={1}, use_global_device_ids=true | all-gather | bytes 81920 | tf_op jit(solution)/shard_map/all_gather | solution.py:46
  775.7 103.0 %all-reduce.16.cloned.1.call-done = (f32[16,4096]{1,0:T(8,128)}, f32[16,4096]{1,0:T(8,128)}, f32[16,4096]{1,0:T(8,128)}, f32[16,4096]{1,0:T(8,128)}) async-done(((f32[16,4096]{1,0:T(8,128)}, f32[16,4096]{1,0:T(8,128)}, f32[16,4096]{1,0:T(8,128)}, f32[16,4096]{1,0:T(8,128)}), (f32[16,4096]{1,0:T(8,128)}, f32[16,4096]{1,0:T(8,128)}, f32[16,4096]{1,0:T(8,128)}, ...) | async-done | bytes 1048592 | tf_op jit(solution)/shard_map/psum | solution.py:51
  879.7 12.7 %all_gather.159 = bf16[16,8192]{1,0:T(8,128)(2,1)S(1)} all-gather(bf16[16,2048]{1,0:T(8,128)(2,1)S(1)} %fusion.120), channel_id=1, replica_groups=mesh['seq'=32,'mp'=4] {'mp'}, dimensions={1}, use_global_device_ids=true | all-gather | bytes 327680 | tf_op jit(solution)/shard_map/all_gather | solution.py:46
  893.5 12.3 %all_gather.149 = bf16[16,8192]{1,0:T(8,128)(2,1)S(1)} all-gather(bf16[16,2048]{1,0:T(8,128)(2,1)S(1)} %fusion.121), channel_id=1, replica_groups=mesh['seq'=32,'mp'=4] {'mp'}, dimensions={1}, use_global_device_ids=true | all-gather | bytes 327680 | tf_op jit(solution)/shard_map/all_gather | solution.py:46
  908.3 12.3 %all_gather.139 = bf16[16,8192]{1,0:T(8,128)(2,1)S(1)} all-gather(bf16[16,2048]{1,0:T(8,128)(2,1)S(1)} %fusion.122), channel_id=1, replica_groups=mesh['seq'=32,'mp'=4] {'mp'}, dimensions={1}, use_global_device_ids=true | all-gather | bytes 327680 | tf_op jit(solution)/shard_map/all_gather | solution.py:46
  922.3 12.3 %all_gather.129 = bf16[16,8192]{1,0:T(8,128)(2,1)S(1)} all-gather(bf16[16,2048]{1,0:T(8,128)(2,1)S(1)} %fusion.123), channel_id=1, replica_groups=mesh['seq'=32,'mp'=4] {'mp'}, dimensions={1}, use_global_device_ids=true | all-gather | bytes 327680 | tf_op jit(solution)/shard_map/all_gather | solution.py:46
  935.4 100.4 %all-reduce.12.cloned.1.call-done = (f32[16,512]{1,0:T(8,128)}, f32[16,512]{1,0:T(8,128)}, f32[16,512]{1,0:T(8,128)}, f32[16,512]{1,0:T(8,128)}) async-done(((f32[16,512]{1,0:T(8,128)}, f32[16,512]{1,0:T(8,128)}, f32[16,512]{1,0:T(8,128)}, f32[16,512]{1,0:T(8,128)}), (f32[16,512]{1,0:T(8,128)}, f32[16,512]{1,0:T(8,128)}, f32[16,512]{1,0:T(8,128)}, f32[16,512]{1,0:T(8,128)})) %all-reduce.12.cloned.1.call-update) | async-done | bytes 131088 | tf_op jit(solution)/shard_map/psum | solution.py:51
  1039.2 10.7 %all-reduce.4 = (f32[16,1]{0,1:T(1,128)S(1)}, f32[16,1]{0,1:T(1,128)S(1)}, f32[16,1]{0,1:T(1,128)S(1)}, f32[16,1]{0,1:T(1,128)S(1)}) all-reduce(f32[16,1]{0,1:T(1,128)S(1)} %bitcast.1052, f32[16,1]{0,1:T(1,128)S(1)} %bitcast.1053, f32[16,1]{0,1:T(1,128)S(1)} %bitcast.1054, ...), channel_id=1, replica_groups=mesh['seq'=32,'mp'=4] {'mp'}, use_global_device_ids=true, to_apply=%region_81.84 | all-reduce | flops 64 | bytes 512 | tf_op jit(solution)/shard_map/psum | solution.py:55
  (1461 shorter events, 176.8 us)
Async XLA Ops:
  6.5 728.6 %copy-start = (bf16[64,2048]{1,0:T(8,128)(2,1)S(1)}, bf16[64,2048]{1,0:T(8,128)(2,1)}, u32[]{:S(2)}) copy-start(bf16[64,2048]{1,0:T(8,128)(2,1)} %param.43) | copy-start | bytes 786436
  6.5 183.6 %copy-start.14 = (s32[16]{0:T(128)S(1)}, s32[16]{0:T(128)}, u32[]{:S(2)}) copy-start(s32[16]{0:T(128)} %param.51) | copy-start | bytes 196
  6.5 183.6 %copy-start.7 = (s32[16]{0:T(128)S(1)}, s32[16]{0:T(128)}, u32[]{:S(2)}) copy-start(s32[16]{0:T(128)} %param.52) | copy-start | bytes 196
  6.5 183.6 %copy-start.15 = (s32[16]{0:T(128)S(1)}, s32[16]{0:T(128)}, u32[]{:S(2)}) copy-start(s32[16]{0:T(128)} %param.53) | copy-start | bytes 196
  6.5 169.6 %all-reduce.18.cloned.1.call-start = ((), (), s32[]{:S(2)}) async-start(), calls=%async_computation.7 | async-start | bytes 786432 | tf_op jit(solution)/shard_map/psum | solution.py:51
  71.1 415.6 %all-gather.27.cloned.1.call-start = ((), (), s32[]{:S(2)}) async-start(), calls=%async_computation.3 | async-start | bytes 1081344 | tf_op jit(solution)/shard_map/all_gather | solution.py:21
  216.5 0.6 copy-start.11
  217.2 284.3 %all-gather.25.cloned.1.call-start = ((), (), s32[]{:S(2)}) async-start(), calls=%async_computation.2 | async-start | bytes 1081344 | tf_op jit(solution)/shard_map/all_gather | solution.py:21
  243.9 0.6 copy-start.10
  270.8 0.6 copy-start.9
  270.9 255.0 %all-gather.23.cloned.1.call-start = ((), (), s32[]{:S(2)}) async-start(), calls=%async_computation.1 | async-start | bytes 1081344 | tf_op jit(solution)/shard_map/all_gather | solution.py:21
  297.8 188.4 %copy-start.8 = (f32[1,16,4,128]{3,1,2,0:T(8,128)}, f32[1,16,4,128]{3,1,2,0:T(8,128)S(1)}, u32[]{:S(2)}) copy-start(f32[1,16,4,128]{3,1,2,0:T(8,128)S(1)} %get-tuple-element.921) | copy-start | bytes 98308
  463.8 39.8 %copy-start.4 = (f32[32,16,4]{1,2,0:T(4,128)}, f32[32,16,4]{1,2,0:T(4,128)S(1)}, u32[]{:S(2)}) copy-start(f32[32,16,4]{1,2,0:T(4,128)S(1)} %all-gather.1) | copy-start | bytes 24580
  485.4 18.3 %copy-start.5 = (f32[32,16,4]{1,2,0:T(4,128)}, f32[32,16,4]{1,2,0:T(4,128)S(1)}, u32[]{:S(2)}) copy-start(f32[32,16,4]{1,2,0:T(4,128)S(1)} %all-gather.2) | copy-start | bytes 24580
  485.9 94.5 %all-gather.21.cloned.1.call-start = ((), (), s32[]{:S(2)}) async-start(), calls=%async_computation | async-start | bytes 1081344 | tf_op jit(solution)/shard_map/all_gather | solution.py:21
  486.5 221.6 %all-reduce.14.cloned.1.call-start = ((), (), s32[]{:S(2)}) async-start(), calls=%async_computation.5 | async-start | bytes 262144 | tf_op jit(solution)/shard_map/psum | solution.py:51
  502.3 75.7 %copy-start.3 = (bf16[64,512]{1,0:T(8,128)(2,1)S(1)}, bf16[64,512]{1,0:T(8,128)(2,1)}, u32[]{:S(2)}) copy-start(bf16[64,512]{1,0:T(8,128)(2,1)} %param.41) | copy-start | bytes 196612
  515.9 66.5 %slice-start = ((f32[32,16,4]{1,2,0:T(4,128)}), f32[1,16,4]{1,2,0:T(4,128)S(1)}, s32[]{:S(2)}) async-start(f32[32,16,4]{1,2,0:T(4,128)} %copy-done.4), calls=%async_computation.8 | async-start | bytes 4096 | tf_op jit(solution)/shard_map/slice | solution.py:22
  515.9 66.5 %slice-start.1 = ((f32[32,16,4]{1,2,0:T(4,128)}), f32[1,16,4]{1,2,0:T(4,128)S(1)}, s32[]{:S(2)}) async-start(f32[32,16,4]{1,2,0:T(4,128)} %copy-done.5), calls=%async_computation.9 | async-start | bytes 4096 | tf_op jit(solution)/shard_map/slice | solution.py:22
  526.7 195.7 %copy-start.6 = (bf16[4,16,512]{2,1,0:T(8,128)(2,1)S(1)}, bf16[4,16,512]{2,1,0:T(8,128)(2,1)}, u32[]{:S(2)}) copy-start(bf16[4,16,512]{2,1,0:T(8,128)(2,1)} %param.37) | copy-start | bytes 196612
  526.7 195.7 %copy-start.12 = (f32[512]{0:T(512)S(1)}, f32[512]{0:T(512)}, u32[]{:S(2)}) copy-start(f32[512]{0:T(512)} %param.47) | copy-start | bytes 6148
  528.0 207.3 %copy-start.1 = (bf16[64,2048]{1,0:T(8,128)(2,1)S(1)}, bf16[64,2048]{1,0:T(8,128)(2,1)}, u32[]{:S(2)}) copy-start(bf16[64,2048]{1,0:T(8,128)(2,1)} %param.42) | copy-start | bytes 786436
  607.9 270.8 %all-reduce.16.cloned.1.call-start = ((), (), s32[]{:S(2)}) async-start(), calls=%async_computation.6 | async-start | bytes 2097152 | tf_op jit(solution)/shard_map/psum | solution.py:51
  709.0 196.8 %copy-start.2 = (bf16[256,512]{1,0:T(8,128)(2,1)S(1)}, bf16[256,512]{1,0:T(8,128)(2,1)}, u32[]{:S(2)}) copy-start(bf16[256,512]{1,0:T(8,128)(2,1)} %param.44) | copy-start | bytes 786436
  760.2 289.7 %copy-start.13 = (f32[512]{0:T(512)S(1)}, f32[512]{0:T(512)}, u32[]{:S(2)}) copy-start(f32[512]{0:T(512)} %param.48) | copy-start | bytes 6148
  775.6 260.1 %all-reduce.12.cloned.1.call-start = ((), (), s32[]{:S(2)}) async-start(), calls=%async_computation.4 | async-start | bytes 262144 | tf_op jit(solution)/shard_map/psum | solution.py:51
Sparse Core Ops, SparseCore 0:
  71.2 104.8 all-reduce.17
  217.3 39.5 all-gather.26
  271.0 39.5 all-gather.24
  486.0 39.8 all-gather.22
  528.0 41.7 all-gather.20
  608.0 100.0 all-reduce.13
  775.7 102.9 all-reduce.15
  935.5 100.2 all-reduce.11
where the time goes:
time: 1060 us
  waiting for transfers between devices  418 us (39%)
  blocking collectives  409 us (39%)
  local copies, waits for them, and re-layouts  86.6 us (8%)
  other arithmetic  64.5 us (6%)
  matrix products  60.8 us (6%)
  between operations  14.4 us (1%)
    psum x4, waiting for transfers between devices, seq_total(): return lax.psum(partial_value, 'seq')  407 us
    all_gather x16, blocking collectives, seq_columns(): gathered = lax.all_gather(token_rows, 'mp', axis=1, tiled=True)  194 us
    all_gather x8, blocking collectives, combined_all(): pieces = jax.tree.map(lambda part: lax.all_gather(part, axis), value)  183 us
    psum x3, blocking collectives, feature_sums(): return lax.psum(squares, 'mp')  32 us
    dot_general x16, matrix products, fold_block(): jnp.einsum('sghd,gthd->sgth', picked, key_block, preferred_element_type=j...  25.4 us
  transfers between devices with their start and end apart: 8, of which 5 were waited for; matrix products, arithmetic and copies ran while one was open for 12% of the time, Pallas kernels for 0%

commit v1 on v0

v1 whole, which is shorter than its diff:
```python
import jax
import jax.numpy as jnp
from jax import lax
from jax.sharding import PartitionSpec as P

D = 2048
HD = 128
R = 16
STEPS = 4
PAGE = 256


epsilon = 1e-06
rope_base = 500000.0
very_low = -1e30


def rotary(values, positions):
    half_width = HD // 2
    frequencies = rope_base ** (-2.0 * jnp.arange(half_width, dtype=jnp.float32) / HD)
    angles = positions.astype(jnp.float32)[:, None] * frequencies[None, :]
    cosine = jnp.cos(angles)[:, None, :]
    sine_part = jnp.sin(angles)[:, None, :]
    first_half = values[..., :half_width]
    second_half = values[..., half_width:]
    return jnp.concatenate(
        [
            first_half * cosine - second_half * sine_part,
            second_half * cosine + first_half * sine_part,
        ],
        axis=-1,
    )


def seq_columns(block, width):
    per = block.shape[1] // width
    seq = lax.axis_index("seq")
    piece = lax.dynamic_slice_in_dim(block, (seq % per) * width, width, 1)
    gathered = lax.all_gather(piece, "mp")
    return lax.dynamic_index_in_dim(gathered, seq // per, 0, keepdims=False)


def seq_total(partial_value):
    return lax.psum(partial_value, "seq")


def feature_sums(squares):
    return lax.psum(squares, "mp")


def inverse_rms(square_total):
    return lax.rsqrt(square_total / D + epsilon)[:, None]


def local(
    states,
    query_weight,
    key_weight,
    value_weight,
    output_weight,
    gate_weight,
    up_weight,
    down_weight,
    query_gain,
    key_gain,
    attention_gain,
    feedforward_gain,
    key_cache,
    value_cache,
    lengths,
    page_owner,
    page_index,
):
    local_width = query_weight.shape[1]
    local_heads = local_width // HD
    rows = STEPS * R
    score_scale = HD ** (-0.5)
    token_rows = states.reshape(rows, local_width)
    positions = (lengths[None, :] + jnp.arange(STEPS, dtype=jnp.int32)[:, None]).reshape(rows)

    sliced = seq_columns(token_rows, query_weight.shape[0])
    summed = seq_total(
        jnp.concatenate(
            [
                jnp.dot(sliced, query_weight, preferred_element_type=jnp.float32),
                jnp.dot(sliced, key_weight, preferred_element_type=jnp.float32),
                jnp.dot(sliced, value_weight, preferred_element_type=jnp.float32),
            ],
            axis=1,
        )
    )
    query_raw = summed[:, :local_width]
    key_raw = summed[:, local_width : 2 * local_width]
    value_raw = summed[:, 2 * local_width :]
    squares = feature_sums(
        jnp.stack([jnp.sum(query_raw * query_raw, axis=1), jnp.sum(key_raw * key_raw, axis=1)], axis=1)
    )
    queries = rotary(
        (query_raw * inverse_rms(squares[:, 0]) * query_gain).reshape(rows, local_heads, HD), positions
    ).astype(jnp.bfloat16)
    new_keys = rotary(
        (key_raw * inverse_rms(squares[:, 1]) * key_gain).reshape(rows, local_heads, HD), positions
    ).astype(jnp.bfloat16)
    new_values = value_raw.astype(jnp.bfloat16).reshape(rows, local_heads, HD)

    pages = key_cache.shape[0]
    tokens = pages * PAGE
    keys = key_cache.reshape(tokens, local_heads, HD)
    values = value_cache.reshape(tokens, local_heads, HD)
    token_owner = jnp.repeat(page_owner, PAGE)
    token_spot = (page_index[:, None] * PAGE + jnp.arange(PAGE, dtype=jnp.int32)[None, :]).reshape(tokens)
    request_of_row = jnp.tile(jnp.arange(R, dtype=jnp.int32), STEPS)
    length_of_row = jnp.tile(lengths, STEPS)
    validity = (token_owner[None, :] == request_of_row[:, None]) & (
        token_spot[None, :] < length_of_row[:, None]
    )
    scores = (
        jnp.einsum("qhd,thd->hqt", queries, keys, preferred_element_type=jnp.float32) * score_scale
    )
    masked = jnp.where(validity[None], scores, very_low)
    maxima = jnp.max(masked, axis=2)
    weights = jnp.where(validity[None], jnp.exp(masked - maxima[..., None]), 0.0)
    totals = jnp.sum(weights, axis=2)
    running = jnp.einsum(
        "hqt,thd->hqd", weights.astype(jnp.bfloat16), values, preferred_element_type=jnp.float32
    )

    all_maxima, all_totals, all_running = lax.all_gather((maxima, totals, running), "seq")
    cache_highest = jnp.max(all_maxima, axis=0)
    scale = jnp.exp(all_maxima - cache_highest[None])
    cache_totals = jnp.sum(all_totals * scale, axis=0)
    cache_running = jnp.sum(all_running * scale[..., None], axis=0)

    q4 = queries.reshape(STEPS, R, local_heads, HD)
    k4 = new_keys.reshape(STEPS, R, local_heads, HD)
    v4 = new_values.reshape(STEPS, R, local_heads, HD)
    fresh_scores = (
        jnp.einsum("srhd,trhd->hsrt", q4, k4, preferred_element_type=jnp.float32) * score_scale
    )
    allowed = (jnp.arange(STEPS)[None, :] <= jnp.arange(STEPS)[:, None])[None, :, None, :]
    fresh_scores = jnp.where(allowed, fresh_scores, very_low)
    cache_highest = cache_highest.reshape(local_heads, STEPS, R)
    highest = jnp.maximum(cache_highest, jnp.max(fresh_scores, axis=-1))
    fresh_weights = jnp.where(allowed, jnp.exp(fresh_scores - highest[..., None]), 0.0)
    factor = jnp.exp(cache_highest - highest)
    final_totals = cache_totals.reshape(local_heads, STEPS, R) * factor + jnp.sum(fresh_weights, axis=-1)
    final_running = cache_running.reshape(local_heads, STEPS, R, HD) * factor[..., None] + jnp.einsum(
        "hsrt,trhd->hsrd", fresh_weights.astype(jnp.bfloat16), v4, preferred_element_type=jnp.float32
    )
    attended = (final_running / final_totals[..., None]).astype(jnp.bfloat16)
    attended = jnp.transpose(attended, (1, 2, 0, 3)).reshape(rows, local_width)

    sliced = seq_columns(attended, output_weight.shape[0])
    attention_out = seq_total(jnp.dot(sliced, output_weight, preferred_element_type=jnp.float32))
    attention_squares = feature_sums(jnp.sum(attention_out * attention_out, axis=1))
    hidden = (
        token_rows.astype(jnp.float32) + attention_out * inverse_rms(attention_squares) * attention_gain
    ).astype(jnp.bfloat16)

    hidden_cols = seq_columns(hidden, gate_weight.shape[0])
    hidden_units = gate_weight.shape[1]
    summed_both = seq_total(
        jnp.concatenate(
            [
                jnp.dot(hidden_cols, gate_weight, preferred_element_type=jnp.float32),
                jnp.dot(hidden_cols, up_weight, preferred_element_type=jnp.float32),
            ],
            axis=1,
        )
    )
    active = (jax.nn.silu(summed_both[:, :hidden_units]) * summed_both[:, hidden_units:]).astype(
        jnp.bfloat16
    )
    active_cols = seq_columns(active, down_weight.shape[0])
    mlp_out = seq_total(jnp.dot(active_cols, down_weight, preferred_element_type=jnp.float32))
    mlp_squares = feature_sums(jnp.sum(mlp_out * mlp_out, axis=1))
    decoded = (
        hidden.astype(jnp.float32) + mlp_out * inverse_rms(mlp_squares) * feedforward_gain
    ).astype(jnp.bfloat16)
    return decoded.reshape(STEPS, R, local_width)


def solution(mesh):
    in_specs = (
        P(None, None, "mp"),
        P("seq", "mp"),
        P("seq", "mp"),
        P("seq", "mp"),
        P("seq", "mp"),
        P("seq", "mp"),
        P("seq", "mp"),
        P("seq", "mp"),
        P("mp"),
        P("mp"),
        P("mp"),
        P("mp"),
        P("seq", None, "mp"),
        P("seq", None, "mp"),
        P(),
        P("seq"),
        P("seq"),
    )
    out_specs = P(None, None, "mp")
    return jax.shard_map(local, mesh=mesh, in_specs=in_specs, out_specs=out_specs, check_vma=False)
```

time: 1060 us -> 583 us (0.55)
  blocking collectives: 409 us -> 128 us
  local copies, waits for them, and re-layouts: 86.6 us -> 21 us
  matrix products: 60.8 us -> 11.8 us
  other arithmetic: 64.5 us -> 17.9 us
  waiting for transfers between devices: 418 us -> 389 us
    all_gather x24 -> x6, blocking collectives: 377 us -> 95.6 us  [the longest x4 49.3 us: seq_columns(): gathered = lax.all_gather(piece, 'mp')]
    dot_general x82 -> x7, matrix products: 52.8 us -> 9.76 us  [the longest x1 4.17 us: local(): jnp.einsum('qhd,thd->hqt', queries, keys, preferred_element_type=jnp.floa...]
    dynamic_slice x140 -> x3, local copies, waits for them, and re-layouts: 22.4 us -> 1 us  [seq_columns(): piece = lax.dynamic_slice_in_dim(block, seq % per * width, width, 1)]
    mul x252 -> x0, local copies, waits for them, and re-layouts: 21 us -> none  [the longest x124 10.4 us: combine_parts(): later_part[2] * second_scale[..., None]]
    gather x32 -> x0, local copies, waits for them, and re-layouts: 18.2 us -> none  [the longest x16 9.17 us: fold_block(): picked = jnp.take(cache_queries, jnp.maximum(owners, 0), axis=1)]
    psum x4, waiting for transfers between devices: 407 us -> 389 us  [seq_total(): return lax.psum(partial_value, 'seq')]
    add x124 -> x1, other arithmetic: 18 us -> 0.01 us  [local(): cache_totals.reshape(local_heads, STEPS, R) * factor]
  transfers between devices with their start and end apart: 8 -> 5, of which waited for: 5 -> 4; matrix products, arithmetic and copies ran while one was open for 12% -> 4% of each run, Pallas kernels for 0% -> 0%
where the time goes in v1:
time: 583 us; the launch traced here: 581 us
  waiting for transfers between devices  389 us (67%)
  blocking collectives  128 us (22%)
  local copies, waits for them, and re-layouts  21 us (4%)
  other arithmetic  17.9 us (3%)
  between operations  13.4 us (2%)
  matrix products  11.8 us (2%)
    psum x4, waiting for transfers between devices, seq_total(): return lax.psum(partial_value, 'seq')  389 us
    all_gather x4, blocking collectives, seq_columns(): gathered = lax.all_gather(piece, 'mp')  49.3 us
    all_gather x2, blocking collectives, local(): lax.all_gather((maxima, totals, running), 'seq')  46.2 us
    psum x3, blocking collectives, feature_sums(): return lax.psum(squares, 'mp')  32 us
  transfers between devices with their start and end apart: 5, of which 4 were waited for; matrix products, arithmetic and copies ran while one was open for 4% of the time, Pallas kernels for 0%

profile of v1, /device:TPU:0, one launch (start us, length us, event | category | flops | bytes accessed | tf_op | source)
XLA Modules:
  0.0 581.3 jit_solution(13567363118520226984)
XLA Ops:
  6.5 0.8 constant_dynamic-slice_fusion.2
  7.4 13.2 %all-gather = bf16[256,64]{1,0:T(8,128)(2,1)S(1)} all-gather(bf16[64,64]{1,0:T(8,128)(2,1)S(1)} %constant_dynamic-slice_fusion.2), channel_id=2, replica_groups=mesh['seq'=32,'mp'=4] {'mp'}, dimensions={0}, use_global_device_ids=true | all-gather | bytes 40960 | tf_op jit(solution)/shard_map/all_gather | solution.py:39
  20.5 1.0 fusion.38
  21.5 1.0 fusion.40
  22.5 1.0 fusion.42
  23.5 0.8 pad_maximum_fusion.1
  24.4 0.7 broadcast_multiply_fusion
  25.0 0.7 tile.5
  25.7 0.1 lt.48
  25.8 0.1 add.125
  25.9 0.1 eq.28
  26.0 0.1 add_bitcast_fusion
  26.1 0.7 broadcast_bitcast_fusion
  26.8 6.9 %reshape.240 = bf16[4096,4,128]{2,1,0:T(4,128)(2,1)} reshape(bf16[16,256,512]{2,1,0:T(8,128)(2,1)} %param.29) | data formatting | bytes 8388608 | tf_op jit(solution)/shard_map/reshape | solution.py:108
  33.7 7.0 %reshape.241 = bf16[4096,4,128]{2,1,0:T(4,128)(2,1)} reshape(bf16[16,256,512]{2,1,0:T(8,128)(2,1)} %param.30) | data formatting | bytes 8388608 | tf_op jit(solution)/shard_map/reshape | solution.py:109
  40.7 0.3 compare_and_fusion
  41.0 0.2 multiply_cosine_fusion
  41.2 87.7 %all-reduce.5.cloned.1.call-done = f32[64,1536]{1,0:T(8,128)} async-done(((f32[64,1536]{1,0:T(8,128)}), f32[64,1536]{1,0:T(8,128)}) %all-reduce.5.cloned.1.call-update) | async-done | bytes 393232 | tf_op jit(solution)/shard_map/psum | solution.py:44
  128.9 1.1 multiply_reduce_fusion.4
  130.0 10.7 %psum.50 = f32[64,2]{0,1:T(2,128)S(1)} all-reduce(f32[64,2]{0,1:T(2,128)S(1)} %pad_maximum_fusion.2), channel_id=1, replica_groups=mesh['seq'=32,'mp'=4] {'mp'}, use_global_device_ids=true, to_apply=%region_3.4 | all-reduce | flops 128 | bytes 1024 | tf_op jit(solution)/shard_map/psum | solution.py:48
  140.7 1.1 multiply_multiply_fusion
  141.9 0.2 fusion.62
  142.1 0.1 subtract_convert_fusion
  142.2 4.2 fusion.64
  146.4 1.9 copy-done.1
  148.3 2.2 fusion.1
  150.5 0.9 slice.62
  151.6 0.3 fusion.20
  151.9 0.2 copy.74
  152.1 0.1 fusion.31
  152.2 0.1 copy.85
  152.3 24.6 %all-gather.7 = f32[32,4,64]{2,1,0:T(4,128)S(1)} all-gather(f32[1,4,64]{2,1,0:T(4,128)S(1)} %bitcast.98), channel_id=4, replica_groups=mesh['seq'=32,'mp'=4] {'seq'}, dimensions={0}, use_global_device_ids=true | all-gather | bytes 33792 | tf_op jit(solution)/shard_map/all_gather | solution.py:128
  177.0 0.1 reshape.243
  177.1 3.2 fusion.4
  180.3 21.6 %all-gather.8 = f32[32,4,64]{2,1,0:T(4,128)S(1)} all-gather(f32[1,4,64]{2,1,0:T(4,128)S(1)} %bitcast.99), channel_id=5, replica_groups=mesh['seq'=32,'mp'=4] {'seq'}, dimensions={0}, use_global_device_ids=true | all-gather | bytes 33792 | tf_op jit(solution)/shard_map/all_gather | solution.py:128
  202.0 0.1 reshape.245
  202.1 0.1 copy.77
  202.2 0.1 copy.79
  202.3 0.1 fusion.50
  202.4 0.1 copy.86
  202.5 0.1 copy.82
  202.6 0.2 copy.81
  202.8 2.9 multiply_reduce_fusion
  205.7 0.2 fusion.13
  206.0 0.1 constant_dynamic-slice_fusion.1
  206.1 11.9 %all-gather.4 = bf16[256,64]{1,0:T(8,128)(2,1)S(1)} all-gather(bf16[64,64]{1,0:T(8,128)(2,1)S(1)} %constant_dynamic-slice_fusion.1), channel_id=6, replica_groups=mesh['seq'=32,'mp'=4] {'mp'}, dimensions={0}, use_global_device_ids=true | all-gather | bytes 40960 | tf_op jit(solution)/shard_map/all_gather | solution.py:39
  218.0 0.8 fusion.36
  218.8 99.1 %all-reduce.7.cloned.1.call-done = f32[64,512]{1,0:T(8,128)} async-done(((f32[64,512]{1,0:T(8,128)}), f32[64,512]{1,0:T(8,128)}) %all-reduce.7.cloned.1.call-update) | async-done | bytes 131088 | tf_op jit(solution)/shard_map/psum | solution.py:44
  317.9 1.0 multiply_reduce_fusion.2
  318.9 10.7 %psum.52 = f32[64]{0:T(128)S(1)} all-reduce(f32[64]{0:T(128)S(1)} %multiply_reduce_fusion.2), channel_id=1, replica_groups=mesh['seq'=32,'mp'=4] {'mp'}, use_global_device_ids=true, to_apply=%region_13.14 | all-reduce | flops 64 | bytes 512 | tf_op jit(solution)/shard_map/psum | solution.py:48
  329.6 1.0 add_convert_fusion.1
  330.6 0.1 constant_dynamic-slice_fusion
  330.7 11.9 %all-gather.5 = bf16[256,64]{1,0:T(8,128)(2,1)S(1)} all-gather(bf16[64,64]{1,0:T(8,128)(2,1)S(1)} %constant_dynamic-slice_fusion), channel_id=7, replica_groups=mesh['seq'=32,'mp'=4] {'mp'}, dimensions={0}, use_global_device_ids=true | all-gather | bytes 40960 | tf_op jit(solution)/shard_map/all_gather | solution.py:39
  342.6 0.2 fusion.32
  342.8 0.2 fusion.34
  343.0 1.1 pad_maximum_fusion
  344.2 102.7 %all-reduce.9.cloned.1.call-done = f32[64,4096]{1,0:T(8,128)} async-done(((f32[64,4096]{1,0:T(8,128)}), f32[64,4096]{1,0:T(8,128)}) %all-reduce.9.cloned.1.call-update) | async-done | bytes 1048592 | tf_op jit(solution)/shard_map/psum | solution.py:44
  446.9 1.4 slice_negate_fusion
  448.3 12.5 %all-gather.6 = bf16[256,256]{1,0:T(8,128)(2,1)S(1)} all-gather(bf16[64,256]{1,0:T(8,128)(2,1)S(1)} %fusion.14), channel_id=8, replica_groups=mesh['seq'=32,'mp'=4] {'mp'}, dimensions={0}, use_global_device_ids=true | all-gather | bytes 163840 | tf_op jit(solution)/shard_map/all_gather | solution.py:39
  460.8 0.8 fusion.28
  461.6 99.8 %all-reduce.11.cloned.1.call-done = f32[64,512]{1,0:T(8,128)} async-done(((f32[64,512]{1,0:T(8,128)}), f32[64,512]{1,0:T(8,128)}) %all-reduce.11.cloned.1.call-update) | async-done | bytes 131088 | tf_op jit(solution)/shard_map/psum | solution.py:44
  561.5 1.0 multiply_reduce_fusion.1
  562.5 10.7 %psum.55 = f32[64]{0:T(128)S(1)} all-reduce(f32[64]{0:T(128)S(1)} %multiply_reduce_fusion.1), channel_id=1, replica_groups=mesh['seq'=32,'mp'=4] {'mp'}, use_global_device_ids=true, to_apply=%region_17.18 | all-reduce | flops 64 | bytes 512 | tf_op jit(solution)/shard_map/psum | solution.py:48
  573.2 1.6 add_convert_fusion
  (57 shorter events, 0.9 us)
Async XLA Ops:
  6.5 336.0 %copy-start = (bf16[64,2048]{1,0:T(8,128)(2,1)S(1)}, bf16[64,2048]{1,0:T(8,128)(2,1)}, u32[]{:S(2)}) copy-start(bf16[64,2048]{1,0:T(8,128)(2,1)} %param.23) | copy-start | bytes 786436
  6.5 122.4 %all-reduce.5.cloned.1.call-start = ((), (), s32[]{:S(2)}) async-start(), calls=%async_computation | async-start | bytes 786432 | tf_op jit(solution)/shard_map/psum | solution.py:44
  24.3 178.5 %all-gather.11.cloned.1.call-start = ((), (), s32[]{:S(2)}) async-start(), calls=%async_computation.4 | async-start | bytes 4325376 | tf_op jit(solution)/shard_map/all_gather | solution.py:128
  33.7 107.0 %copy-start.7 = (f32[512]{0:T(512)S(1)}, f32[512]{0:T(512)}, u32[]{:S(2)}) copy-start(f32[512]{0:T(512)} %param.26) | copy-start | bytes 6148
  33.7 107.0 %copy-start.8 = (f32[512]{0:T(512)S(1)}, f32[512]{0:T(512)}, u32[]{:S(2)}) copy-start(f32[512]{0:T(512)} %param.25) | copy-start | bytes 6148
  142.2 6.1 %copy-start.2 = (bf16[4096,4,128]{2,1,0:T(4,128)(2,1)S(1)}, bf16[4096,4,128]{2,1,0:T(4,128)(2,1)}, u32[]{:S(2)}) copy-start(bf16[4096,4,128]{2,1,0:T(4,128)(2,1)} %reshape.241) | copy-start | bytes 12582916
  146.4 1.9 copy-start.1
  150.5 167.4 %all-reduce.7.cloned.1.call-start = ((), (), s32[]{:S(2)}) async-start(), calls=%async_computation.1 | async-start | bytes 262144 | tf_op jit(solution)/shard_map/psum | solution.py:44
  180.3 37.7 %copy-start.6 = (bf16[64,512]{1,0:T(8,128)(2,1)S(1)}, bf16[64,512]{1,0:T(8,128)(2,1)}, u32[]{:S(2)}) copy-start(bf16[64,512]{1,0:T(8,128)(2,1)} %param.21) | copy-start | bytes 196612
  180.3 149.3 %copy-start.5 = (bf16[4,16,512]{2,1,0:T(8,128)(2,1)S(1)}, bf16[4,16,512]{2,1,0:T(8,128)(2,1)}, u32[]{:S(2)}) copy-start(bf16[4,16,512]{2,1,0:T(8,128)(2,1)} %param.17) | copy-start | bytes 196612
  180.3 149.3 %copy-start.9 = (f32[512]{0:T(512)S(1)}, f32[512]{0:T(512)}, u32[]{:S(2)}) copy-start(f32[512]{0:T(512)} %param.27) | copy-start | bytes 6148
  202.4 140.4 %copy-start.4 = (bf16[64,2048]{1,0:T(8,128)(2,1)S(1)}, bf16[64,2048]{1,0:T(8,128)(2,1)}, u32[]{:S(2)}) copy-start(bf16[64,2048]{1,0:T(8,128)(2,1)} %param.22) | copy-start | bytes 786436
  218.8 242.0 %copy-start.3 = (bf16[256,512]{1,0:T(8,128)(2,1)S(1)}, bf16[256,512]{1,0:T(8,128)(2,1)}, u32[]{:S(2)}) copy-start(bf16[256,512]{1,0:T(8,128)(2,1)} %param.24) | copy-start | bytes 786436
  218.8 228.1 %all-reduce.9.cloned.1.call-start = ((), (), s32[]{:S(2)}) async-start(), calls=%async_computation.2 | async-start | bytes 2097152 | tf_op jit(solution)/shard_map/psum | solution.py:44
  342.6 230.6 %copy-start.10 = (f32[512]{0:T(512)S(1)}, f32[512]{0:T(512)}, u32[]{:S(2)}) copy-start(f32[512]{0:T(512)} %param.28) | copy-start | bytes 6148
  344.1 217.3 %all-reduce.11.cloned.1.call-start = ((), (), s32[]{:S(2)}) async-start(), calls=%async_computation.3 | async-start | bytes 262144 | tf_op jit(solution)/shard_map/psum | solution.py:44
Sparse Core Ops, SparseCore 0:
  24.4 104.4 all-reduce.4
  150.6 42.8 all-gather.10
  218.9 98.9 all-reduce.6
  344.2 102.6 all-reduce.8
  461.8 99.6 all-reduce.10

commit v2 on v1

--- a/solution.py
+++ b/solution.py
@@ -13,6 +13,7 @@
 epsilon = 1e-06
 rope_base = 500000.0
 very_low = -1e30
+SEQ_SIZE = 32
 
 
 def rotary(values, positions):
@@ -41,11 +42,29 @@
 
 
 def seq_total(partial_value):
-    return lax.psum(partial_value, "seq")
+    count = SEQ_SIZE
+    rounds = count.bit_length() - 1
+    me = lax.axis_index("seq")
+    current = partial_value
+    for bit in range(rounds):
+        half = current.shape[1] // 2
+        mine = (me >> bit) & 1
+        keep = lax.dynamic_slice_in_dim(current, mine * half, half, 1)
+        send = lax.dynamic_slice_in_dim(current, (1 - mine) * half, half, 1)
+        pairs = [(i, i ^ (1 << bit)) for i in range(count)]
+        current = keep + lax.ppermute(send, "seq", pairs)
+    for bit in reversed(range(rounds)):
+        mine = (me >> bit) & 1
+        pairs = [(i, i ^ (1 << bit)) for i in range(count)]
+        other = lax.ppermute(current, "seq", pairs)
+        low = jnp.where(mine == 0, current, other)
+        high = jnp.where(mine == 0, other, current)
+        current = jnp.concatenate([low, high], axis=1)
+    return current
 
 
 def feature_sums(squares):
-    return lax.psum(squares, "mp")
+    return jnp.sum(lax.all_gather(squares, "mp"), axis=0)
 
 
 def inverse_rms(square_total):
@@ -105,8 +124,8 @@
 
     pages = key_cache.shape[0]
     tokens = pages * PAGE
-    keys = key_cache.reshape(tokens, local_heads, HD)
-    values = value_cache.reshape(tokens, local_heads, HD)
+    keys = key_cache.reshape(tokens, local_width)
+    values = value_cache.reshape(tokens, local_width)
     token_owner = jnp.repeat(page_owner, PAGE)
     token_spot = (page_index[:, None] * PAGE + jnp.arange(PAGE, dtype=jnp.int32)[None, :]).reshape(tokens)
     request_of_row = jnp.tile(jnp.arange(R, dtype=jnp.int32), STEPS)
@@ -114,15 +133,28 @@
     validity = (token_owner[None, :] == request_of_row[:, None]) & (
         token_spot[None, :] < length_of_row[:, None]
     )
-    scores = (
-        jnp.einsum("qhd,thd->hqt", queries, keys, preferred_element_type=jnp.float32) * score_scale
-    )
+    flat_queries = queries.reshape(rows, local_width)
+    scores = jnp.stack(
+        [
+            lax.dot_general(
+                flat_queries[:, h * HD : (h + 1) * HD],
+                keys[:, h * HD : (h + 1) * HD],
+                (((1,), (1,)), ((), ())),
+                preferred_element_type=jnp.float32,
+            )
+            for h in range(local_heads)
+        ]
+    ) * score_scale
     masked = jnp.where(validity[None], scores, very_low)
     maxima = jnp.max(masked, axis=2)
     weights = jnp.where(validity[None], jnp.exp(masked - maxima[..., None]), 0.0)
     totals = jnp.sum(weights, axis=2)
-    running = jnp.einsum(
-        "hqt,thd->hqd", weights.astype(jnp.bfloat16), values, preferred_element_type=jnp.float32
+    rounded = weights.astype(jnp.bfloat16)
+    running = jnp.stack(
+        [
+            jnp.dot(rounded[h], values[:, h * HD : (h + 1) * HD], preferred_element_type=jnp.float32)
+            for h in range(local_heads)
+        ]
     )
 
     all_maxima, all_totals, all_running = lax.all_gather((maxima, totals, running), "seq")
@@ -181,6 +213,8 @@
 
 
 def solution(mesh):
+    global SEQ_SIZE
+    SEQ_SIZE = mesh.shape["seq"]
     in_specs = (
         P(None, None, "mp"),
         P("seq", "mp"),

time: 583 us -> 340 us (0.58)
  waiting for transfers between devices: 389 us -> 134 us
  starting transfers between devices: 0.17 us -> 38.4 us
  local copies, waits for them, and re-layouts: 21 us -> 7.6 us
  other arithmetic: 17.9 us -> 11.6 us
    psum x4 -> x0, waiting for transfers between devices: 389 us -> none  [seq_total(): return lax.psum(partial_value, 'seq')]
    ppermute x0 -> x40, waiting for transfers between devices: none -> 134 us  [the longest x20 69.3 us: seq_total(): current = keep + lax.ppermute(send, 'seq', pairs)]
    ppermute x0 -> x40, starting transfers between devices: none -> 38.4 us  [the longest x20 19.7 us: seq_total(): current = keep + lax.ppermute(send, 'seq', pairs)]
    psum x3 -> x0, blocking collectives: 32 us -> none  [feature_sums(): return lax.psum(squares, 'mp')]
    unnamed x0 -> x2, blocking collectives: none -> 17.4 us
    reshape x2 -> x0, local copies, waits for them, and re-layouts: 13.9 us -> none  [the longest x1 6.95 us: local(): values = value_cache.reshape(tokens, local_heads, HD)]
    all_gather x0 -> x1, blocking collectives: none -> 9.85 us  [feature_sums(): return jnp.sum(lax.all_gather(squares, 'mp'), axis=0)]
  transfers between devices with their start and end apart: 5 -> 41, of which waited for: 4 -> 39; matrix products, arithmetic and copies ran while one was open for 4% -> 2% of each run, Pallas kernels for 0% -> 0%
where the time goes in v2:
time: 340 us; the launch traced here: 339 us
  waiting for transfers between devices  134 us (39%)
  blocking collectives  124 us (36%)
  starting transfers between devices  38.4 us (11%)
  between operations  14.9 us (4%)
  other arithmetic  11.6 us (3%)
  matrix products  8.67 us (3%)
  local copies, waits for them, and re-layouts  7.6 us (2%)
    ppermute x20, waiting for transfers between devices, seq_total(): current = keep + lax.ppermute(send, 'seq', pairs)  69.3 us
    ppermute x20, waiting for transfers between devices, seq_total(): other = lax.ppermute(current, 'seq', pairs)  64.3 us
    all_gather x4, blocking collectives, seq_columns(): gathered = lax.all_gather(piece, 'mp')  48.9 us
    all_gather x2, blocking collectives, local(): lax.all_gather((maxima, totals, running), 'seq')  48 us
    ppermute x20, starting transfers between devices, seq_total(): current = keep + lax.ppermute(send, 'seq', pairs)  19.7 us
    ppermute x20, starting transfers between devices, seq_total(): other = lax.ppermute(current, 'seq', pairs)  18.7 us
    unnamed x2, blocking collectives  17.4 us
    all_gather x1, blocking collectives, feature_sums(): return jnp.sum(lax.all_gather(squares, 'mp'), axis=0)  9.85 us
  transfers between devices with their start and end apart: 41, of which 39 were waited for; matrix products, arithmetic and copies ran while one was open for 2% of the time, Pallas kernels for 0%

profile of v2, /device:TPU:0, one launch (start us, length us, event | category | flops | bytes accessed | tf_op | source)
XLA Modules:
  0.0 339.1 jit_solution(268023616970309655)
XLA Ops:
  7.4 13.2 %all-gather = bf16[256,64]{1,0:T(8,128)(2,1)S(1)} all-gather(bf16[64,64]{1,0:T(8,128)(2,1)S(1)} %constant_dynamic-slice_fusion.21), channel_id=2, replica_groups=mesh['seq'=32,'mp'=4] {'mp'}, dimensions={0}, use_global_device_ids=true | all-gather | bytes 40960 | tf_op jit(solution)/shard_map/all_gather | solution.py:40
  23.7 1.4 collective-permute-done
  25.2 1.6 collective-permute-start.1
  26.7 3.3 collective-permute-done.1
  30.2 3.1 collective-permute-start.2
  33.3 2.7 collective-permute-done.2
  36.2 1.6 collective-permute-start.3
  38.5 1.7 collective-permute-done.3
  40.3 3.2 collective-permute-start.4
  43.6 2.1 collective-permute-done.4
  45.8 3.2 collective-permute-start.5
  51.5 1.4 collective-permute-start.6
  53.3 2.1 collective-permute-done.6
  55.6 3.1 collective-permute-start.7
  58.7 2.7 collective-permute-done.7
  61.7 1.6 collective-permute-start.8
  63.2 3.1 collective-permute-done.8
  68.2 9.9 %all-gather.10 = f32[4,64,2]{1,2,0:T(2,128)S(1)} all-gather(f32[1,64,2]{1,2,0:T(2,128)S(1)} %maximum_bitcast_fusion.1), channel_id=3, replica_groups=mesh['seq'=32,'mp'=4] {'mp'}, dimensions={0}, use_global_device_ids=true | all-gather | bytes 2560 | tf_op jit(solution)/shard_map/all_gather | solution.py:67
  78.7 1.9 convolution_bitcast_fusion
  82.9 1.4 fusion.1
  87.9 24.4 %all-gather.11 = f32[32,4,64]{2,1,0:T(4,128)S(1)} all-gather(f32[1,4,64]{2,1,0:T(4,128)S(1)} %bitcast.147), channel_id=5, replica_groups=mesh['seq'=32,'mp'=4] {'seq'}, dimensions={0}, use_global_device_ids=true | all-gather | bytes 33792 | tf_op jit(solution)/shard_map/all_gather | solution.py:160
  112.9 23.6 %all-gather.12 = f32[32,4,64]{2,1,0:T(4,128)S(1)} all-gather(f32[1,4,64]{2,1,0:T(4,128)S(1)} %bitcast.148), channel_id=6, replica_groups=mesh['seq'=32,'mp'=4] {'seq'}, dimensions={0}, use_global_device_ids=true | all-gather | bytes 33792 | tf_op jit(solution)/shard_map/all_gather | solution.py:160
  137.1 2.9 multiply_reduce_fusion
  140.4 11.9 %all-gather.5 = bf16[256,64]{1,0:T(8,128)(2,1)S(1)} all-gather(bf16[64,64]{1,0:T(8,128)(2,1)S(1)} %constant_dynamic-slice_fusion.14), channel_id=7, replica_groups=mesh['seq'=32,'mp'=4] {'mp'}, dimensions={0}, use_global_device_ids=true | all-gather | bytes 40960 | tf_op jit(solution)/shard_map/all_gather | solution.py:40
  154.3 3.7 %collective-permute-done.11 = f32[64,128]{1,0:T(8,128)S(1)} collective-permute-done((f32[64,128]{1,0:T(8,128)S(1)}, f32[64,128]{1,0:T(8,128)S(1)}, u32[]{:S(2)}, u32[]{:S(2)}) %collective-permute-start.11) | collective-permute-done | bytes 32800 | tf_op jit(solution)/shard_map/ppermute | solution.py:55
  158.0 1.5 collective-permute-start.12
  159.5 3.9 %collective-permute-done.12 = f32[64,64]{1,0:T(8,128)S(1)} collective-permute-done((f32[64,64]{1,0:T(8,128)S(1)}, f32[64,64]{1,0:T(8,128)S(1)}, u32[]{:S(2)}, u32[]{:S(2)}) %collective-permute-start.12) | collective-permute-done | bytes 16416 | tf_op jit(solution)/shard_map/ppermute | solution.py:55
  163.8 3.8 %collective-permute-done.13 = f32[64,32]{1,0:T(8,128)S(1)} collective-permute-done((f32[64,32]{1,0:T(8,128)S(1)}, f32[64,32]{1,0:T(8,128)S(1)}, u32[]{:S(2)}, u32[]{:S(2)}) %collective-permute-start.13) | collective-permute-done | bytes 8224 | tf_op jit(solution)/shard_map/ppermute | solution.py:55
  167.7 1.5 collective-permute-start.14
  169.2 4.2 %collective-permute-done.14 = f32[64,16]{1,0:T(8,128)S(1)} collective-permute-done((f32[64,16]{1,0:T(8,128)S(1)}, f32[64,16]{1,0:T(8,128)S(1)}, u32[]{:S(2)}, u32[]{:S(2)}) %collective-permute-start.14) | collective-permute-done | bytes 4128 | tf_op jit(solution)/shard_map/ppermute | solution.py:55
  173.4 1.5 collective-permute-start.15
  175.0 3.9 %collective-permute-done.15 = f32[64,16]{1,0:T(8,128)S(1)} collective-permute-done((f32[64,16]{1,0:T(8,128)S(1)}, f32[64,16]{1,0:T(8,128)S(1)}, u32[]{:S(2)}, u32[]{:S(2)}) %collective-permute-start.15) | collective-permute-done | bytes 4128 | tf_op jit(solution)/shard_map/ppermute | solution.py:59
  179.0 3.9 %collective-permute-done.16 = f32[64,32]{1,0:T(8,128)S(1)} collective-permute-done((f32[64,32]{1,0:T(8,128)S(1)}, f32[64,32]{1,0:T(8,128)S(1)}, u32[]{:S(2)}, u32[]{:S(2)}) %collective-permute-start.16) | collective-permute-done | bytes 8224 | tf_op jit(solution)/shard_map/ppermute | solution.py:59
  183.1 1.3 collective-permute-start.17
  184.4 4.2 %collective-permute-done.17 = f32[64,64]{1,0:T(8,128)S(1)} collective-permute-done((f32[64,64]{1,0:T(8,128)S(1)}, f32[64,64]{1,0:T(8,128)S(1)}, u32[]{:S(2)}, u32[]{:S(2)}) %collective-permute-start.17) | collective-permute-done | bytes 16416 | tf_op jit(solution)/shard_map/ppermute | solution.py:59
  188.7 3.9 %collective-permute-done.18 = f32[64,128]{1,0:T(8,128)S(1)} collective-permute-done((f32[64,128]{1,0:T(8,128)S(1)}, f32[64,128]{1,0:T(8,128)S(1)}, u32[]{:S(2)}, u32[]{:S(2)}) %collective-permute-start.18) | collective-permute-done | bytes 32800 | tf_op jit(solution)/shard_map/ppermute | solution.py:59
  194.5 7.7 %all-reduce = f32[256]{0:T(256)S(1)} all-reduce(f32[256]{0:T(256)S(1)} %dynamic-update-slice), channel_id=8, replica_groups=mesh['seq'=32,'mp'=4] {'mp'}, use_global_device_ids=true, to_apply=%add | all-reduce | flops 256 | bytes 2048
  202.5 11.9 %all-gather.7 = bf16[256,64]{1,0:T(8,128)(2,1)S(1)} all-gather(bf16[64,64]{1,0:T(8,128)(2,1)S(1)} %fusion.45), channel_id=9, replica_groups=mesh['seq'=32,'mp'=4] {'mp'}, dimensions={0}, use_global_device_ids=true | all-gather | bytes 40960 | tf_op jit(solution)/shard_map/all_gather | solution.py:40
  215.0 1.9 collective-permute-done.20
  217.1 8.3 %collective-permute-done.21 = f32[64,1024]{1,0:T(8,128)S(1)} collective-permute-done((f32[64,1024]{1,0:T(8,128)S(1)}, f32[64,1024]{1,0:T(8,128)S(1)}, u32[]{:S(2)}, u32[]{:S(2)}) %collective-permute-start.21) | collective-permute-done | bytes 262176 | tf_op jit(solution)/shard_map/ppermute | solution.py:55
  225.5 1.3 collective-permute-start.22
  226.9 5.2 %collective-permute-done.22 = f32[64,512]{1,0:T(8,128)S(1)} collective-permute-done((f32[64,512]{1,0:T(8,128)S(1)}, f32[64,512]{1,0:T(8,128)S(1)}, u32[]{:S(2)}, u32[]{:S(2)}) %collective-permute-start.22) | collective-permute-done | bytes 131104 | tf_op jit(solution)/shard_map/ppermute | solution.py:55
  232.2 4.6 %collective-permute-done.23 = f32[64,256]{1,0:T(8,128)S(1)} collective-permute-done((f32[64,256]{1,0:T(8,128)S(1)}, f32[64,256]{1,0:T(8,128)S(1)}, u32[]{:S(2)}, u32[]{:S(2)}) %collective-permute-start.23) | collective-permute-done | bytes 65568 | tf_op jit(solution)/shard_map/ppermute | solution.py:55
  238.1 4.6 %collective-permute-done.24 = f32[64,128]{1,0:T(8,128)S(1)} collective-permute-done((f32[64,128]{1,0:T(8,128)S(1)}, f32[64,128]{1,0:T(8,128)S(1)}, u32[]{:S(2)}, u32[]{:S(2)}) %collective-permute-start.24) | collective-permute-done | bytes 32800 | tf_op jit(solution)/shard_map/ppermute | solution.py:55
  243.6 4.5 %collective-permute-done.25 = f32[64,128]{1,0:T(8,128)S(1)} collective-permute-done((f32[64,128]{1,0:T(8,128)S(1)}, f32[64,128]{1,0:T(8,128)S(1)}, u32[]{:S(2)}, u32[]{:S(2)}) %collective-permute-start.25) | collective-permute-done | bytes 32800 | tf_op jit(solution)/shard_map/ppermute | solution.py:59
  248.2 4.3 %collective-permute-done.26 = f32[64,256]{1,0:T(8,128)S(1)} collective-permute-done((f32[64,256]{1,0:T(8,128)S(1)}, f32[64,256]{1,0:T(8,128)S(1)}, u32[]{:S(2)}, u32[]{:S(2)}) %collective-permute-start.26) | collective-permute-done | bytes 65568 | tf_op jit(solution)/shard_map/ppermute | solution.py:59
  253.4 5.6 %collective-permute-done.27 = f32[64,512]{1,0:T(8,128)S(1)} collective-permute-done((f32[64,512]{1,0:T(8,128)S(1)}, f32[64,512]{1,0:T(8,128)S(1)}, u32[]{:S(2)}, u32[]{:S(2)}) %collective-permute-start.27) | collective-permute-done | bytes 131104 | tf_op jit(solution)/shard_map/ppermute | solution.py:59
  259.2 6.4 %collective-permute-done.28 = f32[64,1024]{1,0:T(8,128)S(1)} collective-permute-done((f32[64,1024]{1,0:T(8,128)S(1)}, f32[64,1024]{1,0:T(8,128)S(1)}, u32[]{:S(2)}, u32[]{:S(2)}) %collective-permute-start.28) | collective-permute-done | bytes 262176 | tf_op jit(solution)/shard_map/ppermute | solution.py:59
  265.7 1.9 collective-permute-done.29
  267.8 12.0 %all-gather.8 = bf16[256,256]{1,0:T(8,128)(2,1)S(1)} all-gather(bf16[64,256]{1,0:T(8,128)(2,1)S(1)} %fusion.30), channel_id=10, replica_groups=mesh['seq'=32,'mp'=4] {'mp'}, dimensions={0}, use_global_device_ids=true | all-gather | bytes 163840 | tf_op jit(solution)/shard_map/all_gather | solution.py:40
  280.1 1.2 collective-permute-done.30
  281.4 3.9 %collective-permute-done.31 = f32[64,128]{1,0:T(8,128)S(1)} collective-permute-done((f32[64,128]{1,0:T(8,128)S(1)}, f32[64,128]{1,0:T(8,128)S(1)}, u32[]{:S(2)}, u32[]{:S(2)}) %collective-permute-start.31) | collective-permute-done | bytes 32800 | tf_op jit(solution)/shard_map/ppermute | solution.py:55
  285.4 1.3 collective-permute-start.32
  286.7 4.1 %collective-permute-done.32 = f32[64,64]{1,0:T(8,128)S(1)} collective-permute-done((f32[64,64]{1,0:T(8,128)S(1)}, f32[64,64]{1,0:T(8,128)S(1)}, u32[]{:S(2)}, u32[]{:S(2)}) %collective-permute-start.32) | collective-permute-done | bytes 16416 | tf_op jit(solution)/shard_map/ppermute | solution.py:55
  291.3 3.7 %collective-permute-done.33 = f32[64,32]{1,0:T(8,128)S(1)} collective-permute-done((f32[64,32]{1,0:T(8,128)S(1)}, f32[64,32]{1,0:T(8,128)S(1)}, u32[]{:S(2)}, u32[]{:S(2)}) %collective-permute-start.33) | collective-permute-done | bytes 8224 | tf_op jit(solution)/shard_map/ppermute | solution.py:55
  295.1 1.7 collective-permute-start.34
  296.8 3.7 %collective-permute-done.34 = f32[64,16]{1,0:T(8,128)S(1)} collective-permute-done((f32[64,16]{1,0:T(8,128)S(1)}, f32[64,16]{1,0:T(8,128)S(1)}, u32[]{:S(2)}, u32[]{:S(2)}) %collective-permute-start.34) | collective-permute-done | bytes 4128 | tf_op jit(solution)/shard_map/ppermute | solution.py:55
  300.6 1.9 collective-permute-start.35
  302.6 3.5 %collective-permute-done.35 = f32[64,16]{1,0:T(8,128)S(1)} collective-permute-done((f32[64,16]{1,0:T(8,128)S(1)}, f32[64,16]{1,0:T(8,128)S(1)}, u32[]{:S(2)}, u32[]{:S(2)}) %collective-permute-start.35) | collective-permute-done | bytes 4128 | tf_op jit(solution)/shard_map/ppermute | solution.py:59
  306.6 3.5 %collective-permute-done.36 = f32[64,32]{1,0:T(8,128)S(1)} collective-permute-done((f32[64,32]{1,0:T(8,128)S(1)}, f32[64,32]{1,0:T(8,128)S(1)}, u32[]{:S(2)}, u32[]{:S(2)}) %collective-permute-start.36) | collective-permute-done | bytes 8224 | tf_op jit(solution)/shard_map/ppermute | solution.py:59
  310.2 1.4 collective-permute-start.37
  311.7 4.0 %collective-permute-done.37 = f32[64,64]{1,0:T(8,128)S(1)} collective-permute-done((f32[64,64]{1,0:T(8,128)S(1)}, f32[64,64]{1,0:T(8,128)S(1)}, u32[]{:S(2)}, u32[]{:S(2)}) %collective-permute-start.37) | collective-permute-done | bytes 16416 | tf_op jit(solution)/shard_map/ppermute | solution.py:59
  316.1 3.7 %collective-permute-done.38 = f32[64,128]{1,0:T(8,128)S(1)} collective-permute-done((f32[64,128]{1,0:T(8,128)S(1)}, f32[64,128]{1,0:T(8,128)S(1)}, u32[]{:S(2)}, u32[]{:S(2)}) %collective-permute-start.38) | collective-permute-done | bytes 32800 | tf_op jit(solution)/shard_map/ppermute | solution.py:59
  321.6 9.7 %all-reduce.1 = f32[256]{0:T(256)S(1)} all-reduce(f32[256]{0:T(256)S(1)} %dynamic-update-slice.1), channel_id=11, replica_groups=mesh['seq'=32,'mp'=4] {'mp'}, use_global_device_ids=true, to_apply=%add.1 | all-reduce | flops 256 | bytes 2048
  (220 shorter events, 32.2 us)
Async XLA Ops:
  6.5 207.8 %copy-start = (bf16[64,2048]{1,0:T(8,128)(2,1)S(1)}, bf16[64,2048]{1,0:T(8,128)(2,1)}, u32[]{:S(2)}) copy-start(bf16[64,2048]{1,0:T(8,128)(2,1)} %param.23) | copy-start | bytes 786436
  6.5 71.5 %copy-start.6 = (f32[512]{0:T(512)S(1)}, f32[512]{0:T(512)}, u32[]{:S(2)}) copy-start(f32[512]{0:T(512)} %param.26) | copy-start | bytes 6148
  6.5 71.5 %copy-start.7 = (f32[512]{0:T(512)S(1)}, f32[512]{0:T(512)}, u32[]{:S(2)}) copy-start(f32[512]{0:T(512)} %param.25) | copy-start | bytes 6148
  6.5 130.5 %all-gather.15.cloned.1.call-start = ((), (), s32[]{:S(2)}) async-start(), calls=%async_computation | async-start | bytes 4325376 | tf_op jit(solution)/shard_map/all_gather | solution.py:160
  23.6 1.5 collective-permute-start
  25.2 4.9 %collective-permute-start.1 = (f32[64,384]{1,0:T(8,128)S(1)}, f32[64,384]{1,0:T(8,128)S(1)}, u32[]{:S(2)}, u32[]{:S(2)}) collective-permute-start(f32[64,384]{1,0:T(8,128)S(1)} %constant_dynamic-slice_fusion.18), channel_id=1, source_target_pairs={{0,8},{4,12},{8,0},{12,4},{16,24},{20,28},{24,16},{28,20},{32,40},... | collective-permute-start | bytes 294920 | tf_op jit(solution)/shard_map/ppermute | solution.py:55
  30.2 5.8 %collective-permute-start.2 = (f32[64,192]{1,0:T(8,128)S(1)}, f32[64,192]{1,0:T(8,128)S(1)}, u32[]{:S(2)}, u32[]{:S(2)}) collective-permute-start(f32[64,192]{1,0:T(8,128)S(1)} %constant_dynamic-slice_fusion.17), channel_id=1, source_target_pairs={{0,16},{4,20},{8,24},{12,28},{16,0},{20,4},{24,8},{28,12},{32,48},... | collective-permute-start | bytes 147464 | tf_op jit(solution)/shard_map/ppermute | solution.py:55
  36.2 3.9 %collective-permute-start.3 = (f32[64,96]{1,0:T(8,128)S(1)}, f32[64,96]{1,0:T(8,128)S(1)}, u32[]{:S(2)}, u32[]{:S(2)}) collective-permute-start(f32[64,96]{1,0:T(8,128)S(1)} %constant_dynamic-slice_fusion.16), channel_id=1, source_target_pairs={{0,32},{4,36},{8,40},{12,44},{16,48},{20,52},{24,56},{28,60},{32,0... | collective-permute-start | bytes 73736 | tf_op jit(solution)/shard_map/ppermute | solution.py:55
  40.3 5.4 %collective-permute-start.4 = (f32[64,48]{1,0:T(8,128)S(1)}, f32[64,48]{1,0:T(8,128)S(1)}, u32[]{:S(2)}, u32[]{:S(2)}) collective-permute-start(f32[64,48]{1,0:T(8,128)S(1)} %constant_dynamic-slice_fusion.15), channel_id=1, source_target_pairs={{0,64},{4,68},{8,72},{12,76},{16,80},{20,84},{24,88},{28,92},{32,9... | collective-permute-start | bytes 36872 | tf_op jit(solution)/shard_map/ppermute | solution.py:55
  45.8 5.6 %collective-permute-start.5 = (f32[64,48]{1,0:T(8,128)S(1)}, f32[64,48]{1,0:T(8,128)S(1)}, u32[]{:S(2)}, u32[]{:S(2)}) collective-permute-start(f32[64,48]{1,0:T(8,128)S(1)} %dynamic-slice_add_fusion.17), channel_id=1, source_target_pairs={{0,64},{4,68},{8,72},{12,76},{16,80},{20,84},{24,88},{28,92},{32,9... | collective-permute-start | bytes 36872 | tf_op jit(solution)/shard_map/ppermute | solution.py:59
  51.5 3.9 %collective-permute-start.6 = (f32[64,96]{1,0:T(8,128)S(1)}, f32[64,96]{1,0:T(8,128)S(1)}, u32[]{:S(2)}, u32[]{:S(2)}) collective-permute-start(f32[64,96]{1,0:T(8,128)S(1)} %pad_maximum_fusion.13), channel_id=1, source_target_pairs={{0,32},{4,36},{8,40},{12,44},{16,48},{20,52},{24,56},{28,60},{32,0... | collective-permute-start | bytes 73736 | tf_op jit(solution)/shard_map/ppermute | solution.py:59
  55.6 5.8 %collective-permute-start.7 = (f32[64,192]{1,0:T(8,128)S(1)}, f32[64,192]{1,0:T(8,128)S(1)}, u32[]{:S(2)}, u32[]{:S(2)}) collective-permute-start(f32[64,192]{1,0:T(8,128)S(1)} %pad_maximum_fusion.9), channel_id=1, source_target_pairs={{0,16},{4,20},{8,24},{12,28},{16,0},{20,4},{24,8},{28,12},{32,48},... | collective-permute-start | bytes 147464 | tf_op jit(solution)/shard_map/ppermute | solution.py:59
  61.7 4.7 %collective-permute-start.8 = (f32[64,384]{1,0:T(8,128)S(1)}, f32[64,384]{1,0:T(8,128)S(1)}, u32[]{:S(2)}, u32[]{:S(2)}) collective-permute-start(f32[64,384]{1,0:T(8,128)S(1)} %pad_maximum_fusion.8), channel_id=1, source_target_pairs={{0,8},{4,12},{8,0},{12,4},{16,24},{20,28},{24,16},{28,20},{32,40},... | collective-permute-start | bytes 294920 | tf_op jit(solution)/shard_map/ppermute | solution.py:59
  66.5 1.5 collective-permute-start.9
  78.3 2.5 copy-start.1
  82.9 2.2 copy-start.10
  87.2 65.1 %copy-start.5 = (bf16[64,512]{1,0:T(8,128)(2,1)S(1)}, bf16[64,512]{1,0:T(8,128)(2,1)}, u32[]{:S(2)}) copy-start(bf16[64,512]{1,0:T(8,128)(2,1)} %param.21) | copy-start | bytes 196612
  137.0 55.8 %copy-start.8 = (f32[512]{0:T(512)S(1)}, f32[512]{0:T(512)}, u32[]{:S(2)}) copy-start(f32[512]{0:T(512)} %param.27) | copy-start | bytes 6148
  137.0 55.9 %copy-start.11 = (u32[128]{0:T(128)S(1)}, u32[128]{0:T(128)}, u32[]{:S(2)}) copy-start(u32[128]{0:T(128)} %constant.127) | copy-start | bytes 1540
  137.0 65.3 %copy-start.4 = (bf16[4,16,512]{2,1,0:T(8,128)(2,1)S(1)}, bf16[4,16,512]{2,1,0:T(8,128)(2,1)}, u32[]{:S(2)}) copy-start(bf16[4,16,512]{2,1,0:T(8,128)(2,1)} %param.17) | copy-start | bytes 196612
  137.0 77.5 %copy-start.3 = (bf16[64,2048]{1,0:T(8,128)(2,1)S(1)}, bf16[64,2048]{1,0:T(8,128)(2,1)}, u32[]{:S(2)}) copy-start(bf16[64,2048]{1,0:T(8,128)(2,1)} %param.22) | copy-start | bytes 786436
  152.4 1.3 collective-permute-start.10
  153.7 4.2 %collective-permute-start.11 = (f32[64,128]{1,0:T(8,128)S(1)}, f32[64,128]{1,0:T(8,128)S(1)}, u32[]{:S(2)}, u32[]{:S(2)}) collective-permute-start(f32[64,128]{1,0:T(8,128)S(1)} %constant_dynamic-slice_fusion.12), channel_id=1, source_target_pairs={{0,8},{4,12},{8,0},{12,4},{16,24},{20,28},{24,16},{28,20},{32,40},... | collective-permute-start | bytes 98312 | tf_op jit(solution)/shard_map/ppermute | solution.py:55
  158.0 5.4 %collective-permute-start.12 = (f32[64,64]{1,0:T(8,128)S(1)}, f32[64,64]{1,0:T(8,128)S(1)}, u32[]{:S(2)}, u32[]{:S(2)}) collective-permute-start(f32[64,64]{1,0:T(8,128)S(1)} %constant_dynamic-slice_fusion.11), channel_id=1, source_target_pairs={{0,16},{4,20},{8,24},{12,28},{16,0},{20,4},{24,8},{28,12},{32,48},... | collective-permute-start | bytes 49160 | tf_op jit(solution)/shard_map/ppermute | solution.py:55
  163.6 3.9 %collective-permute-start.13 = (f32[64,32]{1,0:T(8,128)S(1)}, f32[64,32]{1,0:T(8,128)S(1)}, u32[]{:S(2)}, u32[]{:S(2)}) collective-permute-start(f32[64,32]{1,0:T(8,128)S(1)} %constant_dynamic-slice_fusion.10), channel_id=1, source_target_pairs={{0,32},{4,36},{8,40},{12,44},{16,48},{20,52},{24,56},{28,60},{32,0... | collective-permute-start | bytes 24584 | tf_op jit(solution)/shard_map/ppermute | solution.py:55
  167.7 5.7 %collective-permute-start.14 = (f32[64,16]{1,0:T(8,128)S(1)}, f32[64,16]{1,0:T(8,128)S(1)}, u32[]{:S(2)}, u32[]{:S(2)}) collective-permute-start(f32[64,16]{1,0:T(8,128)S(1)} %constant_dynamic-slice_fusion.9), channel_id=1, source_target_pairs={{0,64},{4,68},{8,72},{12,76},{16,80},{20,84},{24,88},{28,92},{32,9... | collective-permute-start | bytes 12296 | tf_op jit(solution)/shard_map/ppermute | solution.py:55
  173.4 5.4 %collective-permute-start.15 = (f32[64,16]{1,0:T(8,128)S(1)}, f32[64,16]{1,0:T(8,128)S(1)}, u32[]{:S(2)}, u32[]{:S(2)}) collective-permute-start(f32[64,16]{1,0:T(8,128)S(1)} %dynamic-slice_add_fusion.13), channel_id=1, source_target_pairs={{0,64},{4,68},{8,72},{12,76},{16,80},{20,84},{24,88},{28,92},{32,9... | collective-permute-start | bytes 12296 | tf_op jit(solution)/shard_map/ppermute | solution.py:59
  179.0 3.9 %collective-permute-start.16 = (f32[64,32]{1,0:T(8,128)S(1)}, f32[64,32]{1,0:T(8,128)S(1)}, u32[]{:S(2)}, u32[]{:S(2)}) collective-permute-start(f32[64,32]{1,0:T(8,128)S(1)} %pad_maximum_fusion.14), channel_id=1, source_target_pairs={{0,32},{4,36},{8,40},{12,44},{16,48},{20,52},{24,56},{28,60},{32,0... | collective-permute-start | bytes 24584 | tf_op jit(solution)/shard_map/ppermute | solution.py:59
  183.1 5.4 %collective-permute-start.17 = (f32[64,64]{1,0:T(8,128)S(1)}, f32[64,64]{1,0:T(8,128)S(1)}, u32[]{:S(2)}, u32[]{:S(2)}) collective-permute-start(f32[64,64]{1,0:T(8,128)S(1)} %pad_maximum_fusion.15), channel_id=1, source_target_pairs={{0,16},{4,20},{8,24},{12,28},{16,0},{20,4},{24,8},{28,12},{32,48},... | collective-permute-start | bytes 49160 | tf_op jit(solution)/shard_map/ppermute | solution.py:59
  188.7 3.9 %collective-permute-start.18 = (f32[64,128]{1,0:T(8,128)S(1)}, f32[64,128]{1,0:T(8,128)S(1)}, u32[]{:S(2)}, u32[]{:S(2)}) collective-permute-start(f32[64,128]{1,0:T(8,128)S(1)} %pad_maximum_fusion.16), channel_id=1, source_target_pairs={{0,8},{4,12},{8,0},{12,4},{16,24},{20,28},{24,16},{28,20},{32,40},... | collective-permute-start | bytes 98312 | tf_op jit(solution)/shard_map/ppermute | solution.py:59
  192.7 1.4 collective-permute-start.19
  214.9 2.0 collective-permute-start.20
  217.0 8.4 %collective-permute-start.21 = (f32[64,1024]{1,0:T(8,128)S(1)}, f32[64,1024]{1,0:T(8,128)S(1)}, u32[]{:S(2)}, u32[]{:S(2)}) collective-permute-start(f32[64,1024]{1,0:T(8,128)S(1)} %constant_dynamic-slice_fusion.8), channel_id=1, source_target_pairs={{0,8},{4,12},{8,0},{12,4},{16,24},{20,28},{24,16},{28,20},{32,40},... | collective-permute-start | bytes 786440 | tf_op jit(solution)/shard_map/ppermute | solution.py:55
  225.5 54.3 %copy-start.2 = (bf16[256,512]{1,0:T(8,128)(2,1)S(1)}, bf16[256,512]{1,0:T(8,128)(2,1)}, u32[]{:S(2)}) copy-start(bf16[256,512]{1,0:T(8,128)(2,1)} %param.24) | copy-start | bytes 786436
  225.5 6.6 %collective-permute-start.22 = (f32[64,512]{1,0:T(8,128)S(1)}, f32[64,512]{1,0:T(8,128)S(1)}, u32[]{:S(2)}, u32[]{:S(2)}) collective-permute-start(f32[64,512]{1,0:T(8,128)S(1)} %constant_dynamic-slice_fusion.7), channel_id=1, source_target_pairs={{0,16},{4,20},{8,24},{12,28},{16,0},{20,4},{24,8},{28,12},{32,48},... | collective-permute-start | bytes 393224 | tf_op jit(solution)/shard_map/ppermute | solution.py:55
  232.1 4.7 %collective-permute-start.23 = (f32[64,256]{1,0:T(8,128)S(1)}, f32[64,256]{1,0:T(8,128)S(1)}, u32[]{:S(2)}, u32[]{:S(2)}) collective-permute-start(f32[64,256]{1,0:T(8,128)S(1)} %constant_dynamic-slice_fusion.6), channel_id=1, source_target_pairs={{0,32},{4,36},{8,40},{12,44},{16,48},{20,52},{24,56},{28,60},{32,0... | collective-permute-start | bytes 196616 | tf_op jit(solution)/shard_map/ppermute | solution.py:55
  236.9 5.8 %collective-permute-start.24 = (f32[64,128]{1,0:T(8,128)S(1)}, f32[64,128]{1,0:T(8,128)S(1)}, u32[]{:S(2)}, u32[]{:S(2)}) collective-permute-start(f32[64,128]{1,0:T(8,128)S(1)} %constant_dynamic-slice_fusion.5), channel_id=1, source_target_pairs={{0,64},{4,68},{8,72},{12,76},{16,80},{20,84},{24,88},{28,92},{32,9... | collective-permute-start | bytes 98312 | tf_op jit(solution)/shard_map/ppermute | solution.py:55
  242.6 5.4 %collective-permute-start.25 = (f32[64,128]{1,0:T(8,128)S(1)}, f32[64,128]{1,0:T(8,128)S(1)}, u32[]{:S(2)}, u32[]{:S(2)}) collective-permute-start(f32[64,128]{1,0:T(8,128)S(1)} %dynamic-slice_add_fusion.12), channel_id=1, source_target_pairs={{0,64},{4,68},{8,72},{12,76},{16,80},{20,84},{24,88},{28,92},{32,9... | collective-permute-start | bytes 98312 | tf_op jit(solution)/shard_map/ppermute | solution.py:59
  248.1 4.3 %collective-permute-start.26 = (f32[64,256]{1,0:T(8,128)S(1)}, f32[64,256]{1,0:T(8,128)S(1)}, u32[]{:S(2)}, u32[]{:S(2)}) collective-permute-start(f32[64,256]{1,0:T(8,128)S(1)} %pad_maximum_fusion.11), channel_id=1, source_target_pairs={{0,32},{4,36},{8,40},{12,44},{16,48},{20,52},{24,56},{28,60},{32,0... | collective-permute-start | bytes 196616 | tf_op jit(solution)/shard_map/ppermute | solution.py:59
  252.5 6.6 %collective-permute-start.27 = (f32[64,512]{1,0:T(8,128)S(1)}, f32[64,512]{1,0:T(8,128)S(1)}, u32[]{:S(2)}, u32[]{:S(2)}) collective-permute-start(f32[64,512]{1,0:T(8,128)S(1)} %pad_maximum_fusion.7), channel_id=1, source_target_pairs={{0,16},{4,20},{8,24},{12,28},{16,0},{20,4},{24,8},{28,12},{32,48},... | collective-permute-start | bytes 393224 | tf_op jit(solution)/shard_map/ppermute | solution.py:59
  259.1 72.4 %copy-start.9 = (f32[512]{0:T(512)S(1)}, f32[512]{0:T(512)}, u32[]{:S(2)}) copy-start(f32[512]{0:T(512)} %param.28) | copy-start | bytes 6148
  259.1 6.5 %collective-permute-start.28 = (f32[64,1024]{1,0:T(8,128)S(1)}, f32[64,1024]{1,0:T(8,128)S(1)}, u32[]{:S(2)}, u32[]{:S(2)}) collective-permute-start(f32[64,1024]{1,0:T(8,128)S(1)} %pad_maximum_fusion.2), channel_id=1, source_target_pairs={{0,8},{4,12},{8,0},{12,4},{16,24},{20,28},{24,16},{28,20},{32,40},... | collective-permute-start | bytes 786440 | tf_op jit(solution)/shard_map/ppermute | solution.py:59
  265.6 2.0 collective-permute-start.29
  280.0 1.3 collective-permute-start.30
  281.3 4.0 %collective-permute-start.31 = (f32[64,128]{1,0:T(8,128)S(1)}, f32[64,128]{1,0:T(8,128)S(1)}, u32[]{:S(2)}, u32[]{:S(2)}) collective-permute-start(f32[64,128]{1,0:T(8,128)S(1)} %constant_dynamic-slice_fusion.3), channel_id=1, source_target_pairs={{0,8},{4,12},{8,0},{12,4},{16,24},{20,28},{24,16},{28,20},{32,40},... | collective-permute-start | bytes 98312 | tf_op jit(solution)/shard_map/ppermute | solution.py:55
  285.4 5.4 %collective-permute-start.32 = (f32[64,64]{1,0:T(8,128)S(1)}, f32[64,64]{1,0:T(8,128)S(1)}, u32[]{:S(2)}, u32[]{:S(2)}) collective-permute-start(f32[64,64]{1,0:T(8,128)S(1)} %constant_dynamic-slice_fusion.2), channel_id=1, source_target_pairs={{0,16},{4,20},{8,24},{12,28},{16,0},{20,4},{24,8},{28,12},{32,48},... | collective-permute-start | bytes 49160 | tf_op jit(solution)/shard_map/ppermute | solution.py:55
  291.0 3.9 %collective-permute-start.33 = (f32[64,32]{1,0:T(8,128)S(1)}, f32[64,32]{1,0:T(8,128)S(1)}, u32[]{:S(2)}, u32[]{:S(2)}) collective-permute-start(f32[64,32]{1,0:T(8,128)S(1)} %constant_dynamic-slice_fusion.1), channel_id=1, source_target_pairs={{0,32},{4,36},{8,40},{12,44},{16,48},{20,52},{24,56},{28,60},{32,0... | collective-permute-start | bytes 24584 | tf_op jit(solution)/shard_map/ppermute | solution.py:55
  295.1 5.4 %collective-permute-start.34 = (f32[64,16]{1,0:T(8,128)S(1)}, f32[64,16]{1,0:T(8,128)S(1)}, u32[]{:S(2)}, u32[]{:S(2)}) collective-permute-start(f32[64,16]{1,0:T(8,128)S(1)} %constant_dynamic-slice_fusion), channel_id=1, source_target_pairs={{0,64},{4,68},{8,72},{12,76},{16,80},{20,84},{24,88},{28,92},{32,9... | collective-permute-start | bytes 12296 | tf_op jit(solution)/shard_map/ppermute | solution.py:55
  300.6 5.4 %collective-permute-start.35 = (f32[64,16]{1,0:T(8,128)S(1)}, f32[64,16]{1,0:T(8,128)S(1)}, u32[]{:S(2)}, u32[]{:S(2)}) collective-permute-start(f32[64,16]{1,0:T(8,128)S(1)} %dynamic-slice_add_fusion.8), channel_id=1, source_target_pairs={{0,64},{4,68},{8,72},{12,76},{16,80},{20,84},{24,88},{28,92},{32,9... | collective-permute-start | bytes 12296 | tf_op jit(solution)/shard_map/ppermute | solution.py:59
  306.1 3.9 %collective-permute-start.36 = (f32[64,32]{1,0:T(8,128)S(1)}, f32[64,32]{1,0:T(8,128)S(1)}, u32[]{:S(2)}, u32[]{:S(2)}) collective-permute-start(f32[64,32]{1,0:T(8,128)S(1)} %pad_maximum_fusion.17), channel_id=1, source_target_pairs={{0,32},{4,36},{8,40},{12,44},{16,48},{20,52},{24,56},{28,60},{32,0... | collective-permute-start | bytes 24584 | tf_op jit(solution)/shard_map/ppermute | solution.py:59
  310.2 5.4 %collective-permute-start.37 = (f32[64,64]{1,0:T(8,128)S(1)}, f32[64,64]{1,0:T(8,128)S(1)}, u32[]{:S(2)}, u32[]{:S(2)}) collective-permute-start(f32[64,64]{1,0:T(8,128)S(1)} %pad_maximum_fusion.18), channel_id=1, source_target_pairs={{0,16},{4,20},{8,24},{12,28},{16,0},{20,4},{24,8},{28,12},{32,48},... | collective-permute-start | bytes 49160 | tf_op jit(solution)/shard_map/ppermute | solution.py:59
  315.8 3.9 %collective-permute-start.38 = (f32[64,128]{1,0:T(8,128)S(1)}, f32[64,128]{1,0:T(8,128)S(1)}, u32[]{:S(2)}, u32[]{:S(2)}) collective-permute-start(f32[64,128]{1,0:T(8,128)S(1)} %pad_maximum_fusion.19), channel_id=1, source_target_pairs={{0,8},{4,12},{8,0},{12,4},{16,24},{20,28},{24,16},{28,20},{32,40},... | collective-permute-start | bytes 98312 | tf_op jit(solution)/shard_map/ppermute | solution.py:59
  319.9 1.3 collective-permute-start.39
Sparse Core Ops, SparseCore 0:
  87.1 45.0 all-gather.14
